TPU v7x, 128 devices: a whole 4x4x4 slice. The times are simulated.
128 devices in a mesh: req: 8 (over x, core), hid: 16 (over z, y).
Axes of the slice: x: 4, y: 4, z: 4, core: 2. Of those that a mesh axis runs over, the one named last changes fastest.
Arguments:
- queries: bfloat16 [16, 128, 8192], P('req', None, 'hid'), may hold values from -400 to 400
- suffix_keys: bfloat16 [16, 128, 1024], P('req'), may hold values from -6 to 6
- suffix_values: bfloat16 [16, 128, 1024], P('req'), may hold values from -6 to 6
- prefix_cache: bfloat16 [8192, 2, 1024], P('req'), may hold values from -6 to 6
- prefix_block: int32 [32], replicated, may hold values from 0 to 31, each once
- suffix_len: int32 [16], replicated, may hold values from 1 to 128, 1024 in all
- slot_request: int32 [16], replicated, may hold values from 0 to 15, each once
- residual: bfloat16 [1024, 8192], P(None, 'req'), may hold values from -10 to 10
- out_weight: bfloat16 [8192, 8192], P('hid', 'req'), may hold values from -10 to 10
- post_gain: float32 [8192], P('req'), may hold values from 0.1 to 1.9
- gate_weight: bfloat16 [8192, 28672], P('req', 'hid'), may hold values from -0.0625 to 0.0625
- up_weight: bfloat16 [8192, 28672], P('req', 'hid'), may hold values from -0.0625 to 0.0625
- down_weight: bfloat16 [28672, 8192], P('hid', 'req'), may hold values from -0.03125 to 0.03125
Outputs:
- mixed: bfloat16 [1024, 8192], P('hid', 'req')
Inputs may be any that keep to these rules, and one draw needn't show every extreme that they name: Request i has suffix_len[i] new tokens; they sum to 1024, and the longest has exactly 128. Slot s holds request slot_request[s]; slots r * 2 to (r + 1) * 2 - 1 lie on req index r; every request stands in one slot. Storage rows i * 256 to (i + 1) * 256 - 1 of prefix_cache hold prefix block prefix_block[i]; every block is stored once.
All inputs are finite; a program needn't handle non-finite values.
Results may differ from a plain program's by a relative error of at most 0.019.
Values may be sent and summed in bfloat16 or wider, within the bound.
No kernel may reach another device: no remote copies, remote signals or barrier semaphores. Data moves between devices by JAX's collectives and lax.ppermute only.
A program may use at most 128 MiB of HBM per device.

v0:
```python
import jax
import jax.numpy as jnp
from jax import lax
from jax.sharding import PartitionSpec as P

D = 8192
KVH = 8
HD = 128
PREFIX = 8192
PBLK = 256


ROPE_BASE = 500000.0
EPSILON = 1e-05
MASKED = -1e30


def rotate(vectors, positions):
    half_width = vectors.shape[-1] // 2
    exponent = 2.0 * jnp.arange(half_width, dtype=jnp.float32) / vectors.shape[-1]
    frequency = jnp.exp(-jnp.log(ROPE_BASE) * exponent)
    angles = positions[..., None] * frequency
    cosine = jnp.cos(angles)
    sine_part = jnp.sin(angles)
    lower_half = vectors[..., :half_width]
    upper_half = vectors[..., half_width:]
    return jnp.concatenate(
        [
            lower_half * cosine - upper_half * sine_part,
            upper_half * cosine + lower_half * sine_part,
        ],
        axis=-1,
    )


def slot_lengths(suffix_len, slot_request):
    total_count = suffix_len.shape[0]
    matches = (slot_request[:, None] == jnp.arange(total_count, dtype=jnp.int32)[None, :]).astype(
        jnp.int32
    )
    return jnp.sum(matches * suffix_len[None, :], axis=1)


def token_source(suffix_len, slot_request, tokens, maxlen):
    total_count = suffix_len.shape[0]
    numbers = jnp.arange(total_count, dtype=jnp.int32)
    starts = jnp.cumsum(suffix_len) - suffix_len
    token_ids = jnp.arange(tokens, dtype=jnp.int32)
    reached = (token_ids[:, None] >= starts[None, :]).astype(jnp.int32)
    owner_req = jnp.sum(reached, axis=1) - 1
    onehot = (owner_req[:, None] == numbers[None, :]).astype(jnp.int32)
    start_tok = jnp.sum(onehot * starts[None, :], axis=1)
    inverse = jnp.sum(
        (slot_request[:, None] == numbers[None, :]).astype(jnp.int32) * numbers[:, None], axis=0
    )
    slot_tok = jnp.sum(onehot * inverse[None, :], axis=1)
    return slot_tok * maxlen + token_ids - start_tok


def merge_states(state_one, state_two):
    max_one, total_one, acc_one = state_one
    max_two, total_two, acc_two = state_two
    new_max = jnp.maximum(max_one, max_two)
    shrink_one = jnp.exp(max_one - new_max)
    shrink_two = jnp.exp(max_two - new_max)
    new_total = total_one * shrink_one + total_two * shrink_two
    new_acc = acc_one * shrink_one[:, None] + acc_two * shrink_two[:, None]
    return (new_max, new_total, new_acc)


def on_device(
    queries,
    suffix_keys,
    suffix_values,
    prefix_cache,
    prefix_block,
    suffix_len,
    slot_request,
    residual,
    out_weight,
    post_gain,
    gate_weight,
    up_weight,
    down_weight,
):
    hid_count = lax.axis_size("hid")
    req_count = lax.axis_size("req")
    req_index = lax.axis_index("req")
    hid_index = lax.axis_index("hid")
    local_slots, maxlen, query_cols = queries.shape
    head_count = query_cols // HD
    kv_head = hid_index // (hid_count // KVH)
    scale = HD ** (-0.5)
    all_rows = local_slots * maxlen * head_count
    places = jnp.arange(maxlen, dtype=jnp.int32)
    suffix_pos = (PREFIX + places).astype(jnp.float32)
    query_rot = rotate(
        queries.astype(jnp.float32).reshape(local_slots, maxlen, head_count, HD),
        suffix_pos[None, :, None],
    ).astype(jnp.bfloat16)
    key_cols = lax.dynamic_slice_in_dim(suffix_keys, kv_head * HD, HD, 2)
    key_rot = rotate(key_cols.astype(jnp.float32), suffix_pos[None, :]).astype(jnp.bfloat16)
    value_cols = lax.dynamic_slice_in_dim(suffix_values, kv_head * HD, HD, 2)
    lengths_all = slot_lengths(suffix_len, slot_request)
    local_len = lax.dynamic_slice_in_dim(lengths_all, req_index * local_slots, local_slots, 0)
    allowed = (places[None, :, None] >= places[None, None, :]) & (
        places[None, None, :] < local_len[:, None, None]
    )
    suffix_scores = (
        jnp.einsum("jthd,jud->jthu", query_rot, key_rot, preferred_element_type=jnp.float32) * scale
    )
    suffix_scores = jnp.where(allowed[:, :, None, :], suffix_scores, MASKED)
    suffix_max = jnp.max(suffix_scores, axis=-1)
    suffix_prob = jnp.exp(suffix_scores - suffix_max[..., None])
    suffix_total = jnp.sum(suffix_prob, axis=-1)
    suffix_acc = jnp.einsum(
        "jthu,jud->jthd",
        suffix_prob.astype(jnp.bfloat16),
        value_cols,
        preferred_element_type=jnp.float32,
    )
    suffix_state = (
        suffix_max.reshape(all_rows),
        suffix_total.reshape(all_rows),
        suffix_acc.reshape(all_rows, HD),
    )
    local_prefix = prefix_cache.shape[0]
    block_count = prefix_block.shape[0]
    row_ids = req_index * local_prefix + jnp.arange(local_prefix, dtype=jnp.int32)
    block_match = (
        (row_ids // PBLK)[:, None] == jnp.arange(block_count, dtype=jnp.int32)[None, :]
    ).astype(jnp.int32)
    logical_block = jnp.sum(block_match * prefix_block[None, :], axis=1)
    pre_pos = (logical_block * PBLK + row_ids % PBLK).astype(jnp.float32)
    pre_keys = rotate(
        lax.dynamic_slice_in_dim(prefix_cache[:, 0], kv_head * HD, HD, 1).astype(jnp.float32),
        pre_pos,
    ).astype(jnp.bfloat16)
    pre_values = lax.dynamic_slice_in_dim(prefix_cache[:, 1], kv_head * HD, HD, 1)
    query_flat = query_rot.reshape(all_rows, HD)
    run_max = jnp.full((all_rows,), MASKED, jnp.float32)
    keys_piece = lax.all_gather(pre_keys, "req", axis=0, tiled=True)
    values_piece = lax.all_gather(pre_values, "req", axis=0, tiled=True)
    scores = (
        jnp.einsum("rd,pd->rp", query_flat, keys_piece, preferred_element_type=jnp.float32) * scale
    )
    new_max = jnp.maximum(run_max, jnp.max(scores, axis=1))
    probs = jnp.exp(scores - new_max[:, None])
    new_total = jnp.sum(probs, axis=1)
    new_acc = jnp.dot(probs.astype(jnp.bfloat16), values_piece, preferred_element_type=jnp.float32)
    final_state = (new_max, new_total, new_acc)
    final_state = merge_states(final_state, suffix_state)
    final_max, final_total, final_acc = final_state
    attn_local = (
        (final_acc / final_total[:, None])
        .astype(jnp.bfloat16)
        .reshape(local_slots * maxlen, head_count * HD)
    )
    dealt_rows = jnp.dot(
        lax.all_gather(attn_local, "req", axis=0, tiled=True),
        out_weight,
        preferred_element_type=jnp.float32,
    )
    tokens = residual.shape[0]
    own_rows = tokens // hid_count
    source = token_source(suffix_len, slot_request, tokens, maxlen)
    summed = lax.psum(jnp.take(dealt_rows, source, axis=0).astype(jnp.bfloat16), "hid").astype(
        jnp.float32
    )
    resid_all = (residual.astype(jnp.float32) + summed).astype(jnp.bfloat16)
    resid_own = lax.dynamic_slice_in_dim(resid_all, hid_index * own_rows, own_rows, 0)
    resid_f = lax.optimization_barrier(resid_all).astype(jnp.float32)
    squares = jnp.sum(resid_f * resid_f, axis=1)
    scaled = (resid_f * post_gain[None, :]).astype(jnp.bfloat16)
    gate_part = jnp.dot(scaled, gate_weight, preferred_element_type=jnp.float32)
    up_part = jnp.dot(scaled, up_weight, preferred_element_type=jnp.float32)
    square_all = lax.psum(squares, "req")
    gate_sum, up_sum = (
        lax.psum_scatter(
            gate_part.astype(jnp.bfloat16), "req", scatter_dimension=0, tiled=True
        ).astype(jnp.float32),
        lax.psum_scatter(
            up_part.astype(jnp.bfloat16), "req", scatter_dimension=0, tiled=True
        ).astype(jnp.float32),
    )
    row_count = tokens // req_count
    square_sum = lax.dynamic_slice_in_dim(square_all, req_index * row_count, row_count, 0)
    inv_rms = lax.rsqrt(square_sum / D + EPSILON)
    hidden = (jax.nn.silu(gate_sum * inv_rms[:, None]) * (up_sum * inv_rms[:, None])).astype(
        jnp.bfloat16
    )
    hidden_all = lax.all_gather(hidden, "req", axis=0, tiled=True)
    mixed_rows = lax.psum_scatter(
        jnp.dot(hidden_all, down_weight, preferred_element_type=jnp.float32).astype(jnp.bfloat16),
        "hid",
        scatter_dimension=0,
        tiled=True,
    ).astype(jnp.float32)
    return (resid_own.astype(jnp.float32) + mixed_rows).astype(jnp.bfloat16)


def solution(mesh):
    return jax.shard_map(
        on_device,
        mesh=mesh,
        in_specs=(
            P("req", None, "hid"),
            P("req", None, None),
            P("req", None, None),
            P("req", None, None),
            P(),
            P(),
            P(),
            P(None, "req"),
            P("hid", "req"),
            P("req"),
            P("req", "hid"),
            P("req", "hid"),
            P("hid", "req"),
        ),
        out_specs=P("hid", "req"),
        check_vma=False,
    )
```

profile of v0, /device:TPU:0, one launch (start us, length us, event | category | flops | bytes accessed | tf_op | source)
XLA Modules:
  0.0 433.8 jit_solution(7989682678834533962)
XLA Ops:
  6.6 0.8 select_reduce_fusion
  7.4 10.2 %fusion.69 = (bf16[1024,1,1024]{2,1,0:T(2,128)(2,1)}, bf16[1024,1,1024]{2,1,0:T(2,128)(2,1)}) fusion(bf16[1024,2,1024]{2,1,0:T(2,128)(2,1)} %param.16), kind=kLoop, calls=%fused_computation.108 | loop fusion | bytes 8388608 | tf_op jit(solution)/shard_map/slice | solution.py:136
  17.6 1.6 constant_dynamic-slice_fusion.1
  19.3 0.4 copy.67
  19.7 1.2 fusion.37
  20.8 0.7 pad_maximum_fusion
  21.6 1.6 constant_dynamic-slice_fusion
  23.2 0.7 copy.69
  24.0 0.2 all-gather.8.cloned.1.call-start
  24.3 0.2 select_reduce_fusion.4
  24.6 0.3 multiply_cosine_fusion.1
  24.9 0.9 dynamic-slice_convert_fusion
  25.8 0.2 copy.50
  26.0 0.2 copy.65
  26.2 0.2 copy.64
  26.5 0.2 subtract_convert_fusion
  26.7 0.2 copy.53
  26.9 0.2 copy.54
  27.2 0.3 fusion.71
  27.6 0.1 copy.57
  27.7 1.1 fusion.40
  28.9 0.3 copy.59
  29.2 0.1 reshape.370
  29.4 0.1 copy.60
  29.7 19.8 %all-gather.6.cloned.1.call-done = bf16[8192,128]{0,1:T(8,128)(2,1)} async-done(((bf16[1024,128]{0,1:T(8,128)(2,1)}), bf16[8192,128]{0,1:T(8,128)(2,1)}) %all-gather.6.cloned.1.call-update) | async-done | bytes 2097168 | tf_op jit(solution)/shard_map/all_gather | solution.py:142
  49.5 15.1 %multiply_reduce_fusion = (f32[1024]{0:T(1024)S(1)}, f32[1024,8192]{1,0:T(8,128)}) fusion(bf16[8192,128]{0,1:T(8,128)(2,1)} %all-gather.6.cloned.1.call-done, bf16[1024,64]{1,0:T(8,128)(2,1)S(1)} %bitcast.44, bf16[1024,64]{1,0:T(8,128)(2,1)S(1)} %bitcast.43), kind=kOutput, calls=%fused_computation.2 | convolution fusion | flops 2164784128 | bytes 35917824 | tf_op jit(solution)/shard_map/rd,pd->rp/dot_general | solution.py:145
  64.5 14.2 %fusion = f32[1024]{0:T(1024)S(1)} fusion(f32[1024,8192]{1,0:T(8,128)} %get-tuple-element.25, f32[1024]{0:T(1024)S(1)} %broadcast_maximum_fusion), kind=kLoop, calls=%fused_computation.3 | loop fusion | flops 25164800 | bytes 33562624 | tf_op jit(solution)/shard_map/reduce_sum | solution.py:149
  78.8 14.0 %fusion.25 = bf16[1024,128]{1,0:T(8,128)(2,1)S(1)} fusion(bf16[8192,1,128]{2,0,1:T(8,128)(2,1)} %all-gather.12.cloned.1.call-done, f32[1024,8192]{1,0:T(8,128)} %get-tuple-element.25, f32[1024]{0:T(1024)S(1)} %broadcast_maximum_fusion, f32[1024,128]{1,0:T(8,128)S(1)} %bitcast.45, f32[1024]{0:T(1024)S(1)} %get-tuple-element.9, ...), kind=kOutput, calls=%fused_computation.21 | convolution fusion | flops 2173304832 | bytes 36454400 | tf_op jit(solution)/shard_map/dot_general | solution.py:150
  92.8 0.9 reshape.373
  93.7 0.3 all-reduce.2.cloned.1.call-start
  94.1 0.1 reduce
  94.4 25.0 %all-gather.8.cloned.1.call-done = bf16[2048,512]{1,0:T(8,128)(2,1)} async-done(((bf16[256,512]{1,0:T(8,128)(2,1)}), bf16[2048,512]{1,0:T(8,128)(2,1)}) %all-gather.8.cloned.1.call-update) | async-done | bytes 2097168 | tf_op jit(solution)/shard_map/all_gather | solution.py:160
  119.5 5.9 %fusion.72 = bf16[2048,1024]{1,0:T(8,128)(2,1)} fusion(bf16[2048,512]{1,0:T(8,128)(2,1)} %all-gather.8.cloned.1.call-done, bf16[512,1024]{1,0:T(8,128)(2,1)S(1)} %copy-done), kind=kOutput, calls=%fused_computation.111 | convolution fusion | flops 2147483648 | bytes 7340032 | tf_op jit(solution)/shard_map/dot_general | solution.py:159
  125.3 7.7 %gather_fusion = bf16[1024,1024]{1,0:T(8,128)(2,1)S(1)} fusion(bf16[2048,1024]{1,0:T(8,128)(2,1)} %fusion.72, s32[1024]{0:T(1024)S(1)} %broadcast_clamp_fusion), kind=kCustom, calls=%fused_computation | custom fusion | bytes 4198400 | tf_op jit(solution)/shard_map/jit(_take)/gather | solution.py:167
  133.0 1.7 select_convert_fusion
  134.8 91.8 %all-reduce.2.cloned.1.call-done = bf16[1024,1024]{1,0:T(8,128)(2,1)} async-done(((bf16[1024,1024]{1,0:T(8,128)(2,1)}), bf16[1024,1024]{1,0:T(8,128)(2,1)}) %all-reduce.2.cloned.1.call-update) | async-done | bytes 2097168 | tf_op jit(solution)/shard_map/psum | solution.py:167
  226.7 3.3 add_convert_fusion
  230.1 5.4 %convolution_convert_fusion = bf16[1024,1792]{1,0:T(8,128)(2,1)} fusion(bf16[1024,1792]{1,0:T(8,128)(2,1)S(1)} %copy-done.5, bf16[1024,1024]{1,0:T(8,128)(2,1)S(1)} %add_convert_fusion, f32[1024]{0:T(1024)S(1)} %copy-done.6), kind=kOutput, calls=%fused_computation.12 | convolution fusion | flops 3763077120 | bytes 9441280 | tf_op jit(solution)/shard_map/dot_general | solution.py:176
  235.6 7.5 %convolution_convert_fusion.1 = bf16[1024,1792]{1,0:T(8,128)(2,1)} fusion(bf16[1024,1792]{1,0:T(8,128)(2,1)} %param.23, bf16[1024,1024]{1,0:T(8,128)(2,1)S(1)} %add_convert_fusion, f32[1024]{0:T(1024)S(1)} %copy-done.6), kind=kOutput, calls=%fused_computation.13 | convolution fusion | flops 3763077120 | bytes 9441280 | tf_op jit(solution)/shard_map/dot_general | solution.py:175
  243.1 0.5 fusion.5
  243.6 13.3 %psum.15 = f32[1024]{0:T(1024)S(1)} all-reduce(f32[1024]{0:T(1024)S(1)} %fusion.5), channel_id=1, replica_groups=mesh['req'=8,'hid'=16] {'req'}, use_global_device_ids=true, to_apply=%region_14.15 | all-reduce | flops 1024 | bytes 8192 | tf_op jit(solution)/shard_map/psum | solution.py:177
  257.0 15.0 %reduce-scatter.6.cloned.1.call-done = bf16[128,1792]{1,0:T(8,128)(2,1)} async-done(((bf16[1024,1792]{1,0:T(8,128)(2,1)}), bf16[128,1792]{1,0:T(8,128)(2,1)}) %reduce-scatter.6.cloned.1.call-update) | async-done | bytes 458768 | tf_op jit(solution)/shard_map/reduce_scatter | solution.py:182
  272.0 38.1 %reduce-scatter.4.cloned.1.call-done = bf16[128,1792]{1,0:T(8,128)(2,1)} async-done(((bf16[1024,1792]{1,0:T(8,128)(2,1)}), bf16[128,1792]{1,0:T(8,128)(2,1)}) %reduce-scatter.4.cloned.1.call-update) | async-done | bytes 458768 | tf_op jit(solution)/shard_map/reduce_scatter | solution.py:179
  310.1 2.3 multiply_convert_fusion
  312.5 28.8 %all-gather.10.cloned.1.call-done = bf16[1024,1792]{1,0:T(8,128)(2,1)} async-done(((bf16[128,1792]{1,0:T(8,128)(2,1)}), bf16[1024,1792]{1,0:T(8,128)(2,1)}) %all-gather.10.cloned.1.call-update) | async-done | bytes 3670032 | tf_op jit(solution)/shard_map/all_gather | solution.py:192
  341.3 8.5 %convolution_convert_fusion.2 = bf16[1024,1024]{1,0:T(8,128)(2,1)} fusion(bf16[1024,1792]{1,0:T(8,128)(2,1)} %all-gather.10.cloned.1.call-done, bf16[1792,1024]{1,0:T(8,128)(2,1)} %param.25), kind=kOutput, calls=%fused_computation.15 | convolution fusion | flops 3759144960 | bytes 9437184 | tf_op jit(solution)/shard_map/dot_general | solution.py:194
  349.8 75.5 %reduce-scatter.8.cloned.1.call-done = bf16[64,1024]{1,0:T(8,128)(2,1)} async-done(((bf16[1024,1024]{1,0:T(8,128)(2,1)}), bf16[64,1024]{1,0:T(8,128)(2,1)}) %reduce-scatter.8.cloned.1.call-update) | async-done | bytes 131088 | tf_op jit(solution)/shard_map/reduce_scatter | solution.py:193
  425.3 1.6 add_convert_fusion.2
  (55 shorter events, 1.6 us)
Async XLA Ops:
  6.5 112.9 %copy-start = (bf16[512,1024]{1,0:T(8,128)(2,1)S(1)}, bf16[512,1024]{1,0:T(8,128)(2,1)}, u32[]{:S(2)}) copy-start(bf16[512,1024]{1,0:T(8,128)(2,1)} %param.21) | copy-start | bytes 3145732
  6.5 42.9 %all-gather.6.cloned.1.call-start = ((), (), s32[]{:S(2)}) async-start(), calls=%async_computation.3 | async-start | bytes 2359296 | tf_op jit(solution)/shard_map/all_gather | solution.py:142
  17.6 6.6 %copy-start.3 = (s32[16]{0:T(128)S(1)}, s32[16]{0:T(128)}, u32[]{:S(2)}) copy-start(s32[16]{0:T(128)} %param.18) | copy-start | bytes 196
  17.6 6.7 %copy-start.4 = (s32[16]{0:T(128)S(1)}, s32[16]{0:T(128)}, u32[]{:S(2)}) copy-start(s32[16]{0:T(128)} %param.19) | copy-start | bytes 196
  17.6 8.2 %copy-start.2 = (bf16[2,128,512]{2,1,0:T(8,128)(2,1)S(1)}, bf16[2,128,512]{2,1,0:T(8,128)(2,1)}, u32[]{:S(2)}) copy-start(bf16[2,128,512]{2,1,0:T(8,128)(2,1)} %param.13) | copy-start | bytes 786436
  21.6 57.3 %all-gather.12.cloned.1.call-start = ((), (), s32[]{:S(2)}) async-start(), calls=%async_computation.10 | async-start | bytes 2359296 | tf_op jit(solution)/shard_map/all_gather | solution.py:143
  24.0 95.5 %all-gather.8.cloned.1.call-start = ((), (), s32[]{:S(2)}) async-start(), calls=%async_computation.4 | async-start | bytes 2359296 | tf_op jit(solution)/shard_map/all_gather | solution.py:160
  93.7 133.0 %all-reduce.2.cloned.1.call-start = ((), (), s32[]{:S(2)}) async-start(), calls=%async_computation.5 | async-start | bytes 4194304 | tf_op jit(solution)/shard_map/psum | solution.py:167
  134.8 95.3 %copy-start.6 = (f32[1024]{0:T(1024)S(1)}, f32[1024]{0:T(1024)}, u32[]{:S(2)}) copy-start(f32[1024]{0:T(1024)} %param.22) | copy-start | bytes 12292
  134.8 137.2 %reduce-scatter.6.cloned.1.call-start = ((), (), s32[]{:S(2)}) async-start(), calls=%async_computation.7 | async-start | bytes 4128768 | tf_op jit(solution)/shard_map/reduce_scatter | solution.py:182
  226.7 3.4 copy-start.5
  235.5 74.6 %reduce-scatter.4.cloned.1.call-start = ((), (), s32[]{:S(2)}) async-start(), calls=%async_computation.6 | async-start | bytes 4128768 | tf_op jit(solution)/shard_map/reduce_scatter | solution.py:179
  243.1 98.2 %all-gather.10.cloned.1.call-start = ((), (), s32[]{:S(2)}) async-start(), calls=%async_computation.8 | async-start | bytes 4128768 | tf_op jit(solution)/shard_map/all_gather | solution.py:192
  312.5 112.9 %reduce-scatter.8.cloned.1.call-start = ((), (), s32[]{:S(2)}) async-start(), calls=%async_computation.9 | async-start | bytes 2228224 | tf_op jit(solution)/shard_map/reduce_scatter | solution.py:193
  341.3 85.6 %copy-start.1 = (bf16[512,1024]{1,0:T(8,128)(2,1)S(1)}, bf16[512,1024]{1,0:T(8,128)(2,1)}, u32[]{:S(2)}) copy-start(bf16[512,1024]{1,0:T(8,128)(2,1)} %param.21) | copy-start | bytes 3145732
Sparse Core Ops, SparseCore 0:
  21.7 27.7 all-gather.5
  51.2 25.5 all-gather.11
  93.8 25.6 all-gather.7
  134.9 91.7 all-reduce.1
  235.6 36.3 reduce-scatter.5
  274.3 35.7 reduce-scatter.3
  312.6 28.6 all-gather.9
  349.9 75.3 reduce-scatter.7
where the time goes:
time: 434 us
  waiting for transfers between devices  294 us (68%)
  matrix products  57.8 us (13%)
  other arithmetic  28.8 us (7%)
  local copies, waits for them, and re-layouts  25.1 us (6%)
  between operations  13.8 us (3%)
  blocking collectives  13.3 us (3%)
    psum x1, waiting for transfers between devices, on_device(): lax.psum(jnp.take(dealt_rows, source, axis=0).astype(jnp.bfloat16), 'hid')  91.8 us
    reduce_scatter x1, waiting for transfers between devices, on_device(): lax.psum_scatter(jnp.dot(hidden_all, down_weight, preferred_element_type=...  75.5 us
    reduce_scatter x1, waiting for transfers between devices, on_device(): lax.psum_scatter(gate_part.astype(jnp.bfloat16), 'req', scatter_dimension...  38.1 us
    all_gather x1, waiting for transfers between devices, on_device(): hidden_all = lax.all_gather(hidden, 'req', axis=0, tiled=True)  28.8 us
    all_gather x1, waiting for transfers between devices, on_device(): lax.all_gather(attn_local, 'req', axis=0, tiled=True)  25 us
    all_gather x1, waiting for transfers between devices, on_device(): keys_piece = lax.all_gather(pre_keys, 'req', axis=0, tiled=True)  19.8 us
    dot_general x1, matrix products, on_device(): jnp.einsum('rd,pd->rp', query_flat, keys_piece, preferred_element_type=jn...  15.1 us
    reduce_scatter x1, waiting for transfers between devices, on_device(): lax.psum_scatter(up_part.astype(jnp.bfloat16), 'req', scatter_dimension=0...  15 us
  transfers between devices with their start and end apart: 8, of which 7 were waited for; matrix products, arithmetic and copies ran while one was open for 10% of the time, Pallas kernels for 0%

commit v1 on v0

--- a/solution.py
+++ b/solution.py
@@ -66,6 +66,20 @@
     new_total = total_one * shrink_one + total_two * shrink_two
     new_acc = acc_one * shrink_one[:, None] + acc_two * shrink_two[:, None]
     return (new_max, new_total, new_acc)
+
+
+def exchange_sum(values, axis, count):
+    parts = lax.all_to_all(
+        values.reshape(count, values.shape[0] // count, values.shape[1]), axis, 0, 0, tiled=True
+    )
+    return jnp.sum(parts.astype(jnp.float32), axis=0)
+
+
+def exchange_gather(values, axis, count):
+    parts = lax.all_to_all(
+        jnp.broadcast_to(values[None], (count,) + values.shape), axis, 0, 0, tiled=True
+    )
+    return parts.reshape(count * values.shape[0], values.shape[1])
 
 
 def on_device(
@@ -164,11 +178,12 @@
     tokens = residual.shape[0]
     own_rows = tokens // hid_count
     source = token_source(suffix_len, slot_request, tokens, maxlen)
-    summed = lax.psum(jnp.take(dealt_rows, source, axis=0).astype(jnp.bfloat16), "hid").astype(
-        jnp.float32
-    )
-    resid_all = (residual.astype(jnp.float32) + summed).astype(jnp.bfloat16)
-    resid_own = lax.dynamic_slice_in_dim(resid_all, hid_index * own_rows, own_rows, 0)
+    summed = exchange_sum(
+        jnp.take(dealt_rows, source, axis=0).astype(jnp.bfloat16), "hid", hid_count
+    )
+    residual_own = lax.dynamic_slice_in_dim(residual, hid_index * own_rows, own_rows, 0)
+    resid_own = (residual_own.astype(jnp.float32) + summed).astype(jnp.bfloat16)
+    resid_all = exchange_gather(resid_own, "hid", hid_count)
     resid_f = lax.optimization_barrier(resid_all).astype(jnp.float32)
     squares = jnp.sum(resid_f * resid_f, axis=1)
     scaled = (resid_f * post_gain[None, :]).astype(jnp.bfloat16)
@@ -190,12 +205,11 @@
         jnp.bfloat16
     )
     hidden_all = lax.all_gather(hidden, "req", axis=0, tiled=True)
-    mixed_rows = lax.psum_scatter(
+    mixed_rows = exchange_sum(
         jnp.dot(hidden_all, down_weight, preferred_element_type=jnp.float32).astype(jnp.bfloat16),
         "hid",
-        scatter_dimension=0,
-        tiled=True,
-    ).astype(jnp.float32)
+        hid_count,
+    )
     return (resid_own.astype(jnp.float32) + mixed_rows).astype(jnp.bfloat16)
 
 

time: 434 us -> 368 us (0.85)
  waiting for transfers between devices: 294 us -> 158 us
  blocking collectives: 13.3 us -> 79.2 us
  starting transfers between devices: 0.7 us -> 7.19 us
    psum x1 -> x0, waiting for transfers between devices: 91.8 us -> none  [on_device(): lax.psum(jnp.take(dealt_rows, source, axis=0).astype(jnp.bfloat16), 'hid')]
    reduce_scatter x1 -> x0, waiting for transfers between devices: 75.5 us -> none  [on_device(): lax.psum_scatter(jnp.dot(hidden_all, down_weight, preferred_element_type=...]
    all_to_all x0 -> x2, blocking collectives: none -> 66.7 us  [the longest x1 35.6 us: exchange_sum(): lax.all_to_all(values.reshape(count, values.shape[0] // count, values.sha...]
    all_to_all x0 -> x1, waiting for transfers between devices: none -> 33.4 us  [exchange_sum(): lax.all_to_all(values.reshape(count, values.shape[0] // count, values.sha...]
    all_to_all x0 -> x1, starting transfers between devices: none -> 6.98 us  [exchange_sum(): lax.all_to_all(values.reshape(count, values.shape[0] // count, values.sha...]
  transfers between devices with their start and end apart: 8 -> 7, of which waited for: 7 -> 6; matrix products, arithmetic and copies ran while one was open for 10% -> 12% of each run, Pallas kernels for 0% -> 0%
where the time goes in v1:
time: 368 us; the launch traced here: 367 us
  waiting for transfers between devices  158 us (43%)
  blocking collectives  79.2 us (22%)
  matrix products  56.4 us (15%)
  other arithmetic  26.5 us (7%)
  local copies, waits for them, and re-layouts  25.5 us (7%)
  between operations  13.8 us (4%)
  starting transfers between devices  7.19 us (2%)
    reduce_scatter x1, waiting for transfers between devices, on_device(): lax.psum_scatter(gate_part.astype(jnp.bfloat16), 'req', scatter_dimension...  38.2 us
    all_to_all x1, blocking collectives, exchange_sum(): lax.all_to_all(values.reshape(count, values.shape[0] // count, values.sha...  35.6 us
    all_to_all x1, waiting for transfers between devices, exchange_sum(): lax.all_to_all(values.reshape(count, values.shape[0] // count, values.sha...  33.4 us
    all_to_all x1, blocking collectives, exchange_gather(): lax.all_to_all(jnp.broadcast_to(values[None], (count,) + values.shape), a...  31.2 us
    all_gather x1, waiting for transfers between devices, on_device(): hidden_all = lax.all_gather(hidden, 'req', axis=0, tiled=True)  28.8 us
    all_gather x1, waiting for transfers between devices, on_device(): lax.all_gather(attn_local, 'req', axis=0, tiled=True)  25.1 us
    all_gather x1, waiting for transfers between devices, on_device(): keys_piece = lax.all_gather(pre_keys, 'req', axis=0, tiled=True)  20 us
    dot_general x1, matrix products, on_device(): jnp.einsum('rd,pd->rp', query_flat, keys_piece, preferred_element_type=jn...  15.1 us
  transfers between devices with their start and end apart: 7, of which 6 were waited for; matrix products, arithmetic and copies ran while one was open for 12% of the time, Pallas kernels for 0%

profile of v1, /device:TPU:0, one launch (start us, length us, event | category | flops | bytes accessed | tf_op | source)
XLA Modules:
  0.0 367.2 jit_solution(17204569249957586384)
XLA Ops:
  6.6 0.8 select_reduce_fusion
  7.4 10.2 %fusion.69 = (bf16[1024,1,1024]{2,1,0:T(2,128)(2,1)}, bf16[1024,1,1024]{2,1,0:T(2,128)(2,1)}) fusion(bf16[1024,2,1024]{2,1,0:T(2,128)(2,1)} %param.16), kind=kLoop, calls=%fused_computation.110 | loop fusion | bytes 8388608 | tf_op jit(solution)/shard_map/slice | solution.py:150
  17.6 1.6 constant_dynamic-slice_fusion.1
  19.3 0.4 copy.67
  19.7 1.2 fusion.37
  20.8 0.7 pad_maximum_fusion
  21.6 1.6 constant_dynamic-slice_fusion
  23.2 0.7 copy.69
  24.1 0.2 select_reduce_fusion.4
  24.4 0.3 multiply_cosine_fusion.1
  24.7 0.9 dynamic-slice_convert_fusion
  25.6 0.2 copy.50
  25.8 0.2 copy.65
  26.0 0.2 copy.64
  26.4 0.1 subtract_convert_fusion
  26.5 0.2 copy.53
  26.7 0.2 copy.54
  27.0 0.3 fusion.71
  27.4 0.1 copy.57
  27.5 1.1 fusion.40
  28.7 0.3 copy.59
  29.5 20.0 %all-gather.6.cloned.1.call-done = bf16[8192,128]{0,1:T(8,128)(2,1)} async-done(((bf16[1024,128]{0,1:T(8,128)(2,1)}), bf16[8192,128]{0,1:T(8,128)(2,1)}) %all-gather.6.cloned.1.call-update) | async-done | bytes 2097168 | tf_op jit(solution)/shard_map/all_gather | solution.py:156
  49.5 15.1 %multiply_reduce_fusion = (f32[1024]{0:T(1024)S(1)}, f32[1024,8192]{1,0:T(8,128)}) fusion(bf16[8192,128]{0,1:T(8,128)(2,1)} %all-gather.6.cloned.1.call-done, bf16[1024,64]{1,0:T(8,128)(2,1)S(1)} %bitcast.52, bf16[1024,64]{1,0:T(8,128)(2,1)S(1)} %bitcast.51), kind=kOutput, calls=%fused_computation.2 | convolution fusion | flops 2164784128 | bytes 35917824 | tf_op jit(solution)/shard_map/rd,pd->rp/dot_general | solution.py:159
  64.5 14.2 %fusion = f32[1024]{0:T(1024)S(1)} fusion(f32[1024,8192]{1,0:T(8,128)} %get-tuple-element.25, f32[1024]{0:T(1024)S(1)} %broadcast_maximum_fusion), kind=kLoop, calls=%fused_computation.3 | loop fusion | flops 25164800 | bytes 33562624 | tf_op jit(solution)/shard_map/reduce_sum | solution.py:163
  78.8 14.0 %fusion.25 = bf16[1024,128]{1,0:T(8,128)(2,1)S(1)} fusion(bf16[8192,1,128]{2,0,1:T(8,128)(2,1)} %all-gather.12.cloned.1.call-done, f32[1024,8192]{1,0:T(8,128)} %get-tuple-element.25, f32[1024]{0:T(1024)S(1)} %broadcast_maximum_fusion, f32[1024,128]{1,0:T(8,128)S(1)} %bitcast.53, f32[1024]{0:T(1024)S(1)} %get-tuple-element.9, ...), kind=kOutput, calls=%fused_computation.22 | convolution fusion | flops 2173304832 | bytes 36454400 | tf_op jit(solution)/shard_map/dot_general | solution.py:164
  92.8 0.9 reshape.391
  94.3 25.1 %all-gather.8.cloned.1.call-done = bf16[2048,512]{1,0:T(8,128)(2,1)} async-done(((bf16[256,512]{1,0:T(8,128)(2,1)}), bf16[2048,512]{1,0:T(8,128)(2,1)}) %all-gather.8.cloned.1.call-update) | async-done | bytes 2097168 | tf_op jit(solution)/shard_map/all_gather | solution.py:174
  119.5 5.9 %fusion.72 = bf16[2048,1024]{1,0:T(8,128)(2,1)} fusion(bf16[2048,512]{1,0:T(8,128)(2,1)} %all-gather.8.cloned.1.call-done, bf16[512,1024]{1,0:T(8,128)(2,1)S(1)} %copy-done), kind=kOutput, calls=%fused_computation.113 | convolution fusion | flops 2147483648 | bytes 7340032 | tf_op jit(solution)/shard_map/dot_general | solution.py:173
  125.3 7.7 %gather_fusion = bf16[1024,1024]{1,0:T(8,128)(2,1)S(1)} fusion(bf16[2048,1024]{1,0:T(8,128)(2,1)} %fusion.72, s32[1024]{0:T(1024)S(1)} %broadcast_clamp_fusion), kind=kCustom, calls=%fused_computation | custom fusion | bytes 4198400 | tf_op jit(solution)/shard_map/jit(_take)/gather | solution.py:182
  133.0 1.8 select_convert_fusion
  134.8 7.0 %all-to-all-start = ((bf16[16,64,1024]{2,1,0:T(8,128)(2,1)}), bf16[16,64,1024]{2,1,0:T(8,128)(2,1)S(1)}, u32[]{:S(2)}, u32[]{:S(2)}) async-start(bf16[16,64,1024]{2,1,0:T(8,128)(2,1)} %select_convert_fusion), calls=%async_computation | async-start | bytes 4194304 | tf_op jit(solution)/shard_map/all_to_all | solution.py:72
  141.9 33.4 %all-to-all-done = bf16[16,64,1024]{2,1,0:T(8,128)(2,1)S(1)} async-done(((bf16[16,64,1024]{2,1,0:T(8,128)(2,1)}), bf16[16,64,1024]{2,1,0:T(8,128)(2,1)S(1)}, u32[]{:S(2)}, u32[]{:S(2)}) %all-to-all-start) | async-done | bytes 2097184 | tf_op jit(solution)/shard_map/all_to_all | solution.py:72
  175.2 0.4 convert_reduce_fusion.1
  175.6 1.1 add_convert_fusion.2
  176.7 0.3 broadcast_in_dim.28
  177.0 31.2 %all_to_all.15 = bf16[16,64,1024]{2,1,0:T(8,128)(2,1)S(1)} all-to-all(bf16[16,64,1024]{2,1,0:T(8,128)(2,1)S(1)} %broadcast_in_dim.28), channel_id=1, replica_groups=mesh['req'=8,'hid'=16] {'hid'}, dimensions={0} | all-to-all | bytes 4194304 | tf_op jit(solution)/shard_map/all_to_all | solution.py:79
  208.2 5.4 %convolution_convert_fusion = bf16[1024,1792]{1,0:T(8,128)(2,1)} fusion(bf16[1024,1792]{1,0:T(8,128)(2,1)S(1)} %copy-done.5, bf16[1024,1024]{1,0:T(8,128)(2,1)S(1)} %bitcast.46, f32[1024]{0:T(1024)S(1)} %copy-done.6), kind=kOutput, calls=%fused_computation.13 | convolution fusion | flops 3763077120 | bytes 9441280 | tf_op jit(solution)/shard_map/dot_general | solution.py:191
  213.6 7.5 %convolution_convert_fusion.1 = bf16[1024,1792]{1,0:T(8,128)(2,1)} fusion(bf16[1024,1792]{1,0:T(8,128)(2,1)} %param.23, bf16[1024,1024]{1,0:T(8,128)(2,1)S(1)} %bitcast.47, f32[1024]{0:T(1024)S(1)} %copy-done.6), kind=kOutput, calls=%fused_computation.14 | convolution fusion | flops 3763077120 | bytes 9441280 | tf_op jit(solution)/shard_map/dot_general | solution.py:190
  221.2 0.5 fusion.5
  221.7 12.5 %psum.7 = f32[1024]{0:T(1024)S(1)} all-reduce(f32[1024]{0:T(1024)S(1)} %fusion.5), channel_id=1, replica_groups=mesh['req'=8,'hid'=16] {'req'}, use_global_device_ids=true, to_apply=%region_14.15 | all-reduce | flops 1024 | bytes 8192 | tf_op jit(solution)/shard_map/psum | solution.py:192
  234.3 12.9 %reduce-scatter.5.cloned.1.call-done = bf16[128,1792]{1,0:T(8,128)(2,1)} async-done(((bf16[1024,1792]{1,0:T(8,128)(2,1)}), bf16[128,1792]{1,0:T(8,128)(2,1)}) %reduce-scatter.5.cloned.1.call-update) | async-done | bytes 458768 | tf_op jit(solution)/shard_map/reduce_scatter | solution.py:197
  247.1 38.2 %reduce-scatter.3.cloned.1.call-done = bf16[128,1792]{1,0:T(8,128)(2,1)} async-done(((bf16[1024,1792]{1,0:T(8,128)(2,1)}), bf16[128,1792]{1,0:T(8,128)(2,1)}) %reduce-scatter.3.cloned.1.call-update) | async-done | bytes 458768 | tf_op jit(solution)/shard_map/reduce_scatter | solution.py:194
  285.3 2.3 multiply_convert_fusion
  287.7 28.8 %all-gather.10.cloned.1.call-done = bf16[1024,1792]{1,0:T(8,128)(2,1)} async-done(((bf16[128,1792]{1,0:T(8,128)(2,1)}), bf16[1024,1792]{1,0:T(8,128)(2,1)}) %all-gather.10.cloned.1.call-update) | async-done | bytes 3670032 | tf_op jit(solution)/shard_map/all_gather | solution.py:207
  316.5 7.2 %convolution_convert_fusion.2 = bf16[1024,1024]{1,0:T(8,128)(2,1)S(1)} fusion(bf16[1024,1792]{1,0:T(8,128)(2,1)} %all-gather.10.cloned.1.call-done, bf16[1792,1024]{1,0:T(8,128)(2,1)} %param.25), kind=kOutput, calls=%fused_computation.16 | convolution fusion | flops 3759144960 | bytes 9437184 | tf_op jit(solution)/shard_map/dot_general | solution.py:209
  323.6 35.6 %all_to_all.16 = bf16[16,64,1024]{2,1,0:T(8,128)(2,1)S(1)} all-to-all(bf16[16,64,1024]{2,1,0:T(8,128)(2,1)S(1)} %bitcast.50), channel_id=1, replica_groups=mesh['req'=8,'hid'=16] {'hid'}, dimensions={0} | all-to-all | bytes 4194304 | tf_op jit(solution)/shard_map/all_to_all | solution.py:72
  359.2 0.4 convert_reduce_fusion
  359.6 0.7 add_convert_fusion.1
  (58 shorter events, 2.1 us)
Async XLA Ops:
  6.5 112.9 %copy-start = (bf16[512,1024]{1,0:T(8,128)(2,1)S(1)}, bf16[512,1024]{1,0:T(8,128)(2,1)}, u32[]{:S(2)}) copy-start(bf16[512,1024]{1,0:T(8,128)(2,1)} %param.21) | copy-start | bytes 3145732
  6.5 42.9 %all-gather.6.cloned.1.call-start = ((), (), s32[]{:S(2)}) async-start(), calls=%async_computation.5 | async-start | bytes 2359296 | tf_op jit(solution)/shard_map/all_gather | solution.py:156
  17.6 6.5 %copy-start.3 = (s32[16]{0:T(128)S(1)}, s32[16]{0:T(128)}, u32[]{:S(2)}) copy-start(s32[16]{0:T(128)} %param.18) | copy-start | bytes 196
  17.6 6.5 %copy-start.4 = (s32[16]{0:T(128)S(1)}, s32[16]{0:T(128)}, u32[]{:S(2)}) copy-start(s32[16]{0:T(128)} %param.19) | copy-start | bytes 196
  17.6 8.0 %copy-start.2 = (bf16[2,128,512]{2,1,0:T(8,128)(2,1)S(1)}, bf16[2,128,512]{2,1,0:T(8,128)(2,1)}, u32[]{:S(2)}) copy-start(bf16[2,128,512]{2,1,0:T(8,128)(2,1)} %param.13) | copy-start | bytes 786436
  21.6 57.3 %all-gather.12.cloned.1.call-start = ((), (), s32[]{:S(2)}) async-start(), calls=%async_computation.10 | async-start | bytes 2359296 | tf_op jit(solution)/shard_map/all_gather | solution.py:157
  24.0 95.5 %all-gather.8.cloned.1.call-start = ((), (), s32[]{:S(2)}) async-start(), calls=%async_computation.6 | async-start | bytes 2359296 | tf_op jit(solution)/shard_map/all_gather | solution.py:174
  134.8 40.4 %all-to-all-start = ((bf16[16,64,1024]{2,1,0:T(8,128)(2,1)}), bf16[16,64,1024]{2,1,0:T(8,128)(2,1)S(1)}, u32[]{:S(2)}, u32[]{:S(2)}) async-start(bf16[16,64,1024]{2,1,0:T(8,128)(2,1)} %select_convert_fusion), calls=%async_computation | async-start | bytes 4194304 | tf_op jit(solution)/shard_map/all_to_all | solution.py:72
  141.8 105.3 %reduce-scatter.5.cloned.1.call-start = ((), (), s32[]{:S(2)}) async-start(), calls=%async_computation.8 | async-start | bytes 4128768 | tf_op jit(solution)/shard_map/reduce_scatter | solution.py:197
  175.6 32.6 %copy-start.5 = (bf16[1024,1792]{1,0:T(8,128)(2,1)S(1)}, bf16[1024,1792]{1,0:T(8,128)(2,1)}, u32[]{:S(2)}) copy-start(bf16[1024,1792]{1,0:T(8,128)(2,1)} %param.24) | copy-start | bytes 11010052
  175.6 32.5 %copy-start.6 = (f32[1024]{0:T(1024)S(1)}, f32[1024]{0:T(1024)}, u32[]{:S(2)}) copy-start(f32[1024]{0:T(1024)} %param.22) | copy-start | bytes 12292
  213.6 71.7 %reduce-scatter.3.cloned.1.call-start = ((), (), s32[]{:S(2)}) async-start(), calls=%async_computation.7 | async-start | bytes 4128768 | tf_op jit(solution)/shard_map/reduce_scatter | solution.py:194
  221.2 95.3 %all-gather.10.cloned.1.call-start = ((), (), s32[]{:S(2)}) async-start(), calls=%async_computation.9 | async-start | bytes 4128768 | tf_op jit(solution)/shard_map/all_gather | solution.py:207
  316.5 43.8 %copy-start.1 = (bf16[512,1024]{1,0:T(8,128)(2,1)S(1)}, bf16[512,1024]{1,0:T(8,128)(2,1)}, u32[]{:S(2)}) copy-start(bf16[512,1024]{1,0:T(8,128)(2,1)} %param.21) | copy-start | bytes 3145732
Sparse Core Ops, SparseCore 0:
  21.7 27.7 all-gather.5
  51.2 25.5 all-gather.11
  93.8 25.6 all-gather.7
  213.7 33.3 reduce-scatter.4
  249.4 35.8 reduce-scatter.2
  287.8 28.6 all-gather.9

commit v2 on v1

--- a/solution.py
+++ b/solution.py
@@ -170,17 +170,12 @@
         .astype(jnp.bfloat16)
         .reshape(local_slots * maxlen, head_count * HD)
     )
-    dealt_rows = jnp.dot(
-        lax.all_gather(attn_local, "req", axis=0, tiled=True),
-        out_weight,
-        preferred_element_type=jnp.float32,
-    )
     tokens = residual.shape[0]
     own_rows = tokens // hid_count
     source = token_source(suffix_len, slot_request, tokens, maxlen)
-    summed = exchange_sum(
-        jnp.take(dealt_rows, source, axis=0).astype(jnp.bfloat16), "hid", hid_count
-    )
+    token_rows = jnp.take(lax.all_gather(attn_local, "req", axis=0, tiled=True), source, axis=0)
+    projected = jnp.dot(token_rows, out_weight, preferred_element_type=jnp.float32)
+    summed = exchange_sum(projected.astype(jnp.bfloat16), "hid", hid_count)
     residual_own = lax.dynamic_slice_in_dim(residual, hid_index * own_rows, own_rows, 0)
     resid_own = (residual_own.astype(jnp.float32) + summed).astype(jnp.bfloat16)
     resid_all = exchange_gather(resid_own, "hid", hid_count)
@@ -190,14 +185,14 @@
     gate_part = jnp.dot(scaled, gate_weight, preferred_element_type=jnp.float32)
     up_part = jnp.dot(scaled, up_weight, preferred_element_type=jnp.float32)
     square_all = lax.psum(squares, "req")
-    gate_sum, up_sum = (
-        lax.psum_scatter(
-            gate_part.astype(jnp.bfloat16), "req", scatter_dimension=0, tiled=True
-        ).astype(jnp.float32),
-        lax.psum_scatter(
-            up_part.astype(jnp.bfloat16), "req", scatter_dimension=0, tiled=True
-        ).astype(jnp.float32),
-    )
+    ff_cols = gate_part.shape[1]
+    both_sum = lax.psum_scatter(
+        jnp.concatenate([gate_part.astype(jnp.bfloat16), up_part.astype(jnp.bfloat16)], axis=1),
+        "req",
+        scatter_dimension=0,
+        tiled=True,
+    ).astype(jnp.float32)
+    gate_sum, up_sum = both_sum[:, :ff_cols], both_sum[:, ff_cols:]
     row_count = tokens // req_count
     square_sum = lax.dynamic_slice_in_dim(square_all, req_index * row_count, row_count, 0)
     inv_rms = lax.rsqrt(square_sum / D + EPSILON)

time: 368 us -> 346 us (0.940)
  waiting for transfers between devices: 158 us -> 139 us
  matrix products: 56.4 us -> 51.2 us
  other arithmetic: 26.5 us -> 31.5 us
    reduce_scatter x2 -> x1, waiting for transfers between devices: 51.1 us -> 30.9 us  [on_device(): lax.psum_scatter(jnp.concatenate([gate_part.astype(jnp.bfloat16), up_part...]
    concatenate x0 -> x1, other arithmetic: none -> 6.65 us  [on_device(): jnp.concatenate([gate_part.astype(jnp.bfloat16), up_part.astype(jnp.bfloa...]
  transfers between devices with their start and end apart: 7 -> 6, of which waited for: 6 -> 5; matrix products, arithmetic and copies ran while one was open for 12% -> 11% of each run, Pallas kernels for 0% -> 0%
where the time goes in v2:
time: 346 us; the launch traced here: 345 us
  waiting for transfers between devices  139 us (40%)
  blocking collectives  79.4 us (23%)
  matrix products  51.2 us (15%)
  other arithmetic  31.5 us (9%)
  local copies, waits for them, and re-layouts  23.6 us (7%)
  between operations  13.5 us (4%)
  starting transfers between devices  7.33 us (2%)
    all_to_all x1, blocking collectives, exchange_sum(): lax.all_to_all(values.reshape(count, values.shape[0] // count, values.sha...  35.6 us
    all_to_all x1, waiting for transfers between devices, exchange_sum(): lax.all_to_all(values.reshape(count, values.shape[0] // count, values.sha...  33.3 us
    all_to_all x1, blocking collectives, exchange_gather(): lax.all_to_all(jnp.broadcast_to(values[None], (count,) + values.shape), a...  31.2 us
    reduce_scatter x1, waiting for transfers between devices, on_device(): lax.psum_scatter(jnp.concatenate([gate_part.astype(jnp.bfloat16), up_part...  30.9 us
    all_gather x1, waiting for transfers between devices, on_device(): hidden_all = lax.all_gather(hidden, 'req', axis=0, tiled=True)  29.5 us
    all_gather x1, waiting for transfers between devices, on_device(): lax.all_gather(attn_local, 'req', axis=0, tiled=True)  25.3 us
    all_gather x1, waiting for transfers between devices, on_device(): keys_piece = lax.all_gather(pre_keys, 'req', axis=0, tiled=True)  19.8 us
    dot_general x1, matrix products, on_device(): jnp.einsum('rd,pd->rp', query_flat, keys_piece, preferred_element_type=jn...  15.1 us
  transfers between devices with their start and end apart: 6, of which 5 were waited for; matrix products, arithmetic and copies ran while one was open for 11% of the time, Pallas kernels for 0%

profile of v2, /device:TPU:0, one launch (start us, length us, event | category | flops | bytes accessed | tf_op | source)
XLA Modules:
  0.0 345.4 jit_solution(8684600165784300709)
XLA Ops:
  6.6 0.8 select_reduce_fusion
  7.4 10.2 %fusion.75 = (bf16[1024,1,1024]{2,1,0:T(2,128)(2,1)}, bf16[1024,1,1024]{2,1,0:T(2,128)(2,1)}) fusion(bf16[1024,2,1024]{2,1,0:T(2,128)(2,1)} %param.16), kind=kLoop, calls=%fused_computation.118 | loop fusion | bytes 8388608 | tf_op jit(solution)/shard_map/slice | solution.py:150
  17.6 1.6 constant_dynamic-slice_fusion.1
  19.3 0.4 copy.67
  19.7 1.2 fusion.42
  20.8 0.7 pad_maximum_fusion.1
  21.6 1.6 constant_dynamic-slice_fusion
  23.2 0.7 copy.69
  24.0 0.2 all-gather.8.cloned.1.call-start
  24.3 0.2 select_reduce_fusion.4
  24.6 0.3 multiply_cosine_fusion.1
  24.9 0.9 dynamic-slice_convert_fusion
  25.8 0.2 copy.50
  26.0 0.2 copy.65
  26.2 0.2 copy.64
  26.5 0.2 subtract_convert_fusion
  26.7 0.2 copy.53
  26.9 0.2 copy.54
  27.2 0.3 fusion.77
  27.7 1.1 fusion.45
  28.9 0.3 copy.59
  29.7 19.8 %all-gather.6.cloned.1.call-done = bf16[8192,128]{0,1:T(8,128)(2,1)} async-done(((bf16[1024,128]{0,1:T(8,128)(2,1)}), bf16[8192,128]{0,1:T(8,128)(2,1)}) %all-gather.6.cloned.1.call-update) | async-done | bytes 2097168 | tf_op jit(solution)/shard_map/all_gather | solution.py:156
  49.5 15.1 %multiply_reduce_fusion = (f32[1024]{0:T(1024)S(1)}, f32[1024,8192]{1,0:T(8,128)}) fusion(bf16[8192,128]{0,1:T(8,128)(2,1)} %all-gather.6.cloned.1.call-done, bf16[1024,64]{1,0:T(8,128)(2,1)S(1)} %bitcast.51, bf16[1024,64]{1,0:T(8,128)(2,1)S(1)} %bitcast.50), kind=kOutput, calls=%fused_computation.2 | convolution fusion | flops 2164784128 | bytes 35917824 | tf_op jit(solution)/shard_map/rd,pd->rp/dot_general | solution.py:159
  64.5 14.2 %fusion = f32[1024]{0:T(1024)S(1)} fusion(f32[1024,8192]{1,0:T(8,128)} %get-tuple-element.25, f32[1024]{0:T(1024)S(1)} %broadcast_maximum_fusion), kind=kLoop, calls=%fused_computation.3 | loop fusion | flops 25164800 | bytes 33562624 | tf_op jit(solution)/shard_map/reduce_sum | solution.py:163
  78.8 14.0 %fusion.25 = bf16[1024,128]{1,0:T(8,128)(2,1)S(1)} fusion(bf16[8192,1,128]{2,0,1:T(8,128)(2,1)} %all-gather.12.cloned.1.call-done, f32[1024,8192]{1,0:T(8,128)} %get-tuple-element.25, f32[1024]{0:T(1024)S(1)} %broadcast_maximum_fusion, f32[1024,128]{1,0:T(8,128)S(1)} %bitcast.52, f32[1024]{0:T(1024)S(1)} %get-tuple-element.9, ...), kind=kOutput, calls=%fused_computation.23 | convolution fusion | flops 2173304832 | bytes 36454400 | tf_op jit(solution)/shard_map/dot_general | solution.py:164
  92.8 0.9 reshape.383
  94.2 25.3 %all-gather.8.cloned.1.call-done = bf16[2048,512]{1,0:T(8,128)(2,1)} async-done(((bf16[256,512]{1,0:T(8,128)(2,1)}), bf16[2048,512]{1,0:T(8,128)(2,1)}) %all-gather.8.cloned.1.call-update) | async-done | bytes 2097168 | tf_op jit(solution)/shard_map/all_gather | solution.py:176
  119.5 5.8 %gather_fusion = bf16[1024,512]{1,0:T(8,128)(2,1)S(1)} fusion(bf16[2048,512]{1,0:T(8,128)(2,1)} %all-gather.8.cloned.1.call-done, s32[1024]{0:T(1024)S(1)} %broadcast_clamp_fusion), kind=kCustom, calls=%fused_computation | custom fusion | bytes 2101248 | tf_op jit(solution)/shard_map/jit(_take)/gather | solution.py:176
  125.4 2.7 convolution_convert_fusion.3
  128.0 7.0 %all-to-all-start = ((bf16[16,64,1024]{2,1,0:T(8,128)(2,1)}), bf16[16,64,1024]{2,1,0:T(8,128)(2,1)S(1)}, u32[]{:S(2)}, u32[]{:S(2)}) async-start(bf16[16,64,1024]{2,1,0:T(8,128)(2,1)} %bitcast.48), calls=%async_computation | async-start | bytes 4194304 | tf_op jit(solution)/shard_map/all_to_all | solution.py:72
  135.1 33.3 %all-to-all-done = bf16[16,64,1024]{2,1,0:T(8,128)(2,1)S(1)} async-done(((bf16[16,64,1024]{2,1,0:T(8,128)(2,1)}), bf16[16,64,1024]{2,1,0:T(8,128)(2,1)S(1)}, u32[]{:S(2)}, u32[]{:S(2)}) %all-to-all-start) | async-done | bytes 2097184 | tf_op jit(solution)/shard_map/all_to_all | solution.py:72
  168.4 0.4 convert_reduce_fusion.1
  168.8 1.1 add_convert_fusion.2
  169.9 0.3 broadcast_in_dim.28
  170.2 31.2 %all_to_all.15 = bf16[16,64,1024]{2,1,0:T(8,128)(2,1)S(1)} all-to-all(bf16[16,64,1024]{2,1,0:T(8,128)(2,1)S(1)} %broadcast_in_dim.28), channel_id=1, replica_groups=mesh['req'=8,'hid'=16] {'hid'}, dimensions={0} | all-to-all | bytes 4194304 | tf_op jit(solution)/shard_map/all_to_all | solution.py:79
  201.3 5.4 %convolution_convert_fusion = bf16[1024,1792]{1,0:T(8,128)(2,1)} fusion(bf16[1024,1792]{1,0:T(8,128)(2,1)S(1)} %copy-done.5, bf16[1024,1024]{1,0:T(8,128)(2,1)S(1)} %bitcast.44, f32[1024]{0:T(1024)S(1)} %copy-done.7), kind=kOutput, calls=%fused_computation.13 | convolution fusion | flops 3763077120 | bytes 9441280 | tf_op jit(solution)/shard_map/dot_general | solution.py:186
  206.8 5.4 %convolution_convert_fusion.1 = bf16[1024,1792]{1,0:T(8,128)(2,1)} fusion(bf16[1024,1792]{1,0:T(8,128)(2,1)S(1)} %copy-done.6, bf16[1024,1024]{1,0:T(8,128)(2,1)S(1)} %bitcast.45, f32[1024]{0:T(1024)S(1)} %copy-done.7), kind=kOutput, calls=%fused_computation.14 | convolution fusion | flops 3763077120 | bytes 9441280 | tf_op jit(solution)/shard_map/dot_general | solution.py:185
  212.2 6.6 %pad_maximum_fusion = bf16[1024,3584]{1,0:T(8,128)(2,1)} fusion(bf16[1024,1792]{1,0:T(8,128)(2,1)} %convolution_convert_fusion, bf16[1024,1792]{1,0:T(8,128)(2,1)} %convolution_convert_fusion.1), kind=kLoop, calls=%fused_computation.6 | loop fusion | flops 14680064 | bytes 14680064 | tf_op jit(solution)/shard_map/concatenate | solution.py:190
  218.9 0.5 fusion.5
  219.4 12.6 %psum.7 = f32[1024]{0:T(1024)S(1)} all-reduce(f32[1024]{0:T(1024)S(1)} %fusion.5), channel_id=1, replica_groups=mesh['req'=8,'hid'=16] {'req'}, use_global_device_ids=true, to_apply=%region_14.15 | all-reduce | flops 1024 | bytes 8192 | tf_op jit(solution)/shard_map/psum | solution.py:187
  232.1 30.9 %reduce-scatter.2.cloned.1.call-done = bf16[128,3584]{1,0:T(8,128)(2,1)} async-done(((bf16[1024,3584]{1,0:T(8,128)(2,1)}), bf16[128,3584]{1,0:T(8,128)(2,1)}) %reduce-scatter.2.cloned.1.call-update) | async-done | bytes 917520 | tf_op jit(solution)/shard_map/reduce_scatter | solution.py:189
  263.0 1.4 convert_element_type.122
  264.4 1.1 fusion.33
  265.5 29.5 %all-gather.10.cloned.1.call-done = bf16[1024,1792]{1,0:T(8,128)(2,1)} async-done(((bf16[128,1792]{1,0:T(8,128)(2,1)}), bf16[1024,1792]{1,0:T(8,128)(2,1)}) %all-gather.10.cloned.1.call-update) | async-done | bytes 3670032 | tf_op jit(solution)/shard_map/all_gather | solution.py:202
  295.0 7.2 %convolution_convert_fusion.2 = bf16[1024,1024]{1,0:T(8,128)(2,1)S(1)} fusion(bf16[1024,1792]{1,0:T(8,128)(2,1)} %all-gather.10.cloned.1.call-done, bf16[1792,1024]{1,0:T(8,128)(2,1)} %param.25), kind=kOutput, calls=%fused_computation.16 | convolution fusion | flops 3759144960 | bytes 9437184 | tf_op jit(solution)/shard_map/dot_general | solution.py:204
  302.2 35.6 %all_to_all.16 = bf16[16,64,1024]{2,1,0:T(8,128)(2,1)S(1)} all-to-all(bf16[16,64,1024]{2,1,0:T(8,128)(2,1)S(1)} %bitcast.49), channel_id=1, replica_groups=mesh['req'=8,'hid'=16] {'hid'}, dimensions={0} | all-to-all | bytes 4194304 | tf_op jit(solution)/shard_map/all_to_all | solution.py:72
  337.8 0.4 convert_reduce_fusion
  338.2 0.7 add_convert_fusion.1
  (56 shorter events, 2.0 us)
Async XLA Ops:
  6.5 118.8 %copy-start = (bf16[512,1024]{1,0:T(8,128)(2,1)S(1)}, bf16[512,1024]{1,0:T(8,128)(2,1)}, u32[]{:S(2)}) copy-start(bf16[512,1024]{1,0:T(8,128)(2,1)} %param.21) | copy-start | bytes 3145732
  6.5 42.9 %all-gather.6.cloned.1.call-start = ((), (), s32[]{:S(2)}) async-start(), calls=%async_computation.4 | async-start | bytes 2359296 | tf_op jit(solution)/shard_map/all_gather | solution.py:156
  17.6 6.6 %copy-start.3 = (s32[16]{0:T(128)S(1)}, s32[16]{0:T(128)}, u32[]{:S(2)}) copy-start(s32[16]{0:T(128)} %param.18) | copy-start | bytes 196
  17.6 6.7 %copy-start.4 = (s32[16]{0:T(128)S(1)}, s32[16]{0:T(128)}, u32[]{:S(2)}) copy-start(s32[16]{0:T(128)} %param.19) | copy-start | bytes 196
  17.6 8.2 %copy-start.2 = (bf16[2,128,512]{2,1,0:T(8,128)(2,1)S(1)}, bf16[2,128,512]{2,1,0:T(8,128)(2,1)}, u32[]{:S(2)}) copy-start(bf16[2,128,512]{2,1,0:T(8,128)(2,1)} %param.13) | copy-start | bytes 786436
  21.6 57.3 %all-gather.12.cloned.1.call-start = ((), (), s32[]{:S(2)}) async-start(), calls=%async_computation.8 | async-start | bytes 2359296 | tf_op jit(solution)/shard_map/all_gather | solution.py:157
  24.0 95.5 %all-gather.8.cloned.1.call-start = ((), (), s32[]{:S(2)}) async-start(), calls=%async_computation.5 | async-start | bytes 2359296 | tf_op jit(solution)/shard_map/all_gather | solution.py:176
  128.0 40.4 %all-to-all-start = ((bf16[16,64,1024]{2,1,0:T(8,128)(2,1)}), bf16[16,64,1024]{2,1,0:T(8,128)(2,1)S(1)}, u32[]{:S(2)}, u32[]{:S(2)}) async-start(bf16[16,64,1024]{2,1,0:T(8,128)(2,1)} %bitcast.48), calls=%async_computation | async-start | bytes 4194304 | tf_op jit(solution)/shard_map/all_to_all | solution.py:72
  135.0 128.0 %reduce-scatter.2.cloned.1.call-start = ((), (), s32[]{:S(2)}) async-start(), calls=%async_computation.6 | async-start | bytes 8257536 | tf_op jit(solution)/shard_map/reduce_scatter | solution.py:189
  168.8 32.5 %copy-start.5 = (bf16[1024,1792]{1,0:T(8,128)(2,1)S(1)}, bf16[1024,1792]{1,0:T(8,128)(2,1)}, u32[]{:S(2)}) copy-start(bf16[1024,1792]{1,0:T(8,128)(2,1)} %param.24) | copy-start | bytes 11010052
  168.8 32.5 %copy-start.7 = (f32[1024]{0:T(1024)S(1)}, f32[1024]{0:T(1024)}, u32[]{:S(2)}) copy-start(f32[1024]{0:T(1024)} %param.22) | copy-start | bytes 12292
  201.3 5.4 %copy-start.6 = (bf16[1024,1792]{1,0:T(8,128)(2,1)S(1)}, bf16[1024,1792]{1,0:T(8,128)(2,1)}, u32[]{:S(2)}) copy-start(bf16[1024,1792]{1,0:T(8,128)(2,1)} %param.23) | copy-start | bytes 11010052
  218.9 76.2 %all-gather.10.cloned.1.call-start = ((), (), s32[]{:S(2)}) async-start(), calls=%async_computation.7 | async-start | bytes 4128768 | tf_op jit(solution)/shard_map/all_gather | solution.py:202
  295.0 43.8 %copy-start.1 = (bf16[512,1024]{1,0:T(8,128)(2,1)S(1)}, bf16[512,1024]{1,0:T(8,128)(2,1)}, u32[]{:S(2)}) copy-start(bf16[512,1024]{1,0:T(8,128)(2,1)} %param.21) | copy-start | bytes 3145732
Sparse Core Ops, SparseCore 0:
  21.7 27.7 all-gather.5
  51.2 25.5 all-gather.11
  93.8 25.6 all-gather.7
  219.0 43.9 reduce-scatter.1
  265.6 29.3 all-gather.9

commit v3 on v2

--- a/solution.py
+++ b/solution.py
@@ -1,6 +1,8 @@
 import jax
 import jax.numpy as jnp
 from jax import lax
+from jax.experimental import pallas as pl
+from jax.experimental.pallas import tpu as pltpu
 from jax.sharding import PartitionSpec as P
 
 D = 8192
@@ -80,6 +82,52 @@
         jnp.broadcast_to(values[None], (count,) + values.shape), axis, 0, 0, tiled=True
     )
     return parts.reshape(count * values.shape[0], values.shape[1])
+
+
+def prefix_kernel(q_ref, k_ref, v_ref, m_ref, l_ref, acc_ref):
+    @pl.when(pl.program_id(1) == 0)
+    def _():
+        m_ref[...] = jnp.full(m_ref.shape, MASKED, jnp.float32)
+        l_ref[...] = jnp.zeros(l_ref.shape, jnp.float32)
+        acc_ref[...] = jnp.zeros(acc_ref.shape, jnp.float32)
+
+    scores = lax.dot_general(
+        q_ref[...], k_ref[...], (((1,), (1,)), ((), ())), preferred_element_type=jnp.float32
+    ) * (HD ** (-0.5))
+    m_prev = m_ref[...]
+    m_new = jnp.maximum(m_prev, jnp.max(scores, axis=1, keepdims=True))
+    shrink = jnp.exp(m_prev - m_new)
+    probs = jnp.exp(scores - m_new)
+    l_ref[...] = shrink * l_ref[...] + jnp.sum(probs, axis=1, keepdims=True)
+    acc_ref[...] = shrink * acc_ref[...] + jnp.dot(
+        probs.astype(jnp.bfloat16), v_ref[...], preferred_element_type=jnp.float32
+    )
+    m_ref[...] = m_new
+
+
+def prefix_attention(query_flat, keys, values, q_tile=512, k_tile=1024):
+    rows = query_flat.shape[0]
+    length = keys.shape[0]
+    return pl.pallas_call(
+        prefix_kernel,
+        out_shape=(
+            jax.ShapeDtypeStruct((rows, 1), jnp.float32),
+            jax.ShapeDtypeStruct((rows, 1), jnp.float32),
+            jax.ShapeDtypeStruct((rows, HD), jnp.float32),
+        ),
+        grid=(rows // q_tile, length // k_tile),
+        in_specs=[
+            pl.BlockSpec((q_tile, HD), lambda i, j: (i, 0)),
+            pl.BlockSpec((k_tile, HD), lambda i, j: (j, 0)),
+            pl.BlockSpec((k_tile, HD), lambda i, j: (j, 0)),
+        ],
+        out_specs=(
+            pl.BlockSpec((q_tile, 1), lambda i, j: (i, 0)),
+            pl.BlockSpec((q_tile, 1), lambda i, j: (i, 0)),
+            pl.BlockSpec((q_tile, HD), lambda i, j: (i, 0)),
+        ),
+        compiler_params=pltpu.CompilerParams(dimension_semantics=("parallel", "arbitrary")),
+    )(query_flat, keys, values)
 
 
 def on_device(
@@ -152,17 +200,10 @@
     ).astype(jnp.bfloat16)
     pre_values = lax.dynamic_slice_in_dim(prefix_cache[:, 1], kv_head * HD, HD, 1)
     query_flat = query_rot.reshape(all_rows, HD)
-    run_max = jnp.full((all_rows,), MASKED, jnp.float32)
     keys_piece = lax.all_gather(pre_keys, "req", axis=0, tiled=True)
     values_piece = lax.all_gather(pre_values, "req", axis=0, tiled=True)
-    scores = (
-        jnp.einsum("rd,pd->rp", query_flat, keys_piece, preferred_element_type=jnp.float32) * scale
-    )
-    new_max = jnp.maximum(run_max, jnp.max(scores, axis=1))
-    probs = jnp.exp(scores - new_max[:, None])
-    new_total = jnp.sum(probs, axis=1)
-    new_acc = jnp.dot(probs.astype(jnp.bfloat16), values_piece, preferred_element_type=jnp.float32)
-    final_state = (new_max, new_total, new_acc)
+    new_max, new_total, new_acc = prefix_attention(query_flat, keys_piece, values_piece)
+    final_state = (new_max.reshape(all_rows), new_total.reshape(all_rows), new_acc)
     final_state = merge_states(final_state, suffix_state)
     final_max, final_total, final_acc = final_state
     attn_local = (

time: 346 us -> 367 us (1.061)
  Pallas kernels: 0 us -> 32.4 us
  matrix products: 51.2 us -> 22.2 us
  waiting for transfers between devices: 139 us -> 166 us
  other arithmetic: 31.5 us -> 22.7 us
    pallas_call x0 -> x1, Pallas kernels: none -> 32.4 us  [prefix_attention(): pl.pallas_call(prefix_kernel, out_shape=(jax.ShapeDtypeStruct((rows, 1),...]
    dot_general x2 -> x0, matrix products: 29 us -> none  [the longest x1 15.1 us: on_device(): jnp.einsum('rd,pd->rp', query_flat, keys_piece, preferred_element_type=jn...]
    all_gather x1, waiting for transfers between devices: 0.02 us -> 27.4 us  [on_device(): values_piece = lax.all_gather(pre_values, 'req', axis=0, tiled=True)]
    reduce_sum x1 -> x0, other arithmetic: 14.2 us -> none  [on_device(): new_total = jnp.sum(probs, axis=1)]
  transfers between devices with their start and end apart: 6 -> 6, of which waited for: 5 -> 6; matrix products, arithmetic and copies ran while one was open for 11% -> 3% of each run, Pallas kernels for 0% -> 0%
where the time goes in v3:
time: 367 us; the launch traced here: 366 us
  waiting for transfers between devices  166 us (45%)
  blocking collectives  79.6 us (22%)
  Pallas kernels  32.4 us (9%)
  local copies, waits for them, and re-layouts  23.3 us (6%)
  other arithmetic  22.7 us (6%)
  matrix products  22.2 us (6%)
  between operations  13.5 us (4%)
  starting transfers between devices  7.15 us (2%)
    all_to_all x1, blocking collectives, exchange_sum(): lax.all_to_all(values.reshape(count, values.shape[0] // count, values.sha...  35.6 us
    all_to_all x1, waiting for transfers between devices, exchange_sum(): lax.all_to_all(values.reshape(count, values.shape[0] // count, values.sha...  33.4 us
    pallas_call x1, Pallas kernels, prefix_attention(): pl.pallas_call(prefix_kernel, out_shape=(jax.ShapeDtypeStruct((rows, 1),...  32.4 us
    all_to_all x1, blocking collectives, exchange_gather(): lax.all_to_all(jnp.broadcast_to(values[None], (count,) + values.shape), a...  31.4 us
    reduce_scatter x1, waiting for transfers between devices, on_device(): lax.psum_scatter(jnp.concatenate([gate_part.astype(jnp.bfloat16), up_part...  30.8 us
    all_gather x1, waiting for transfers between devices, on_device(): hidden_all = lax.all_gather(hidden, 'req', axis=0, tiled=True)  29.5 us
    all_gather x1, waiting for transfers between devices, on_device(): values_piece = lax.all_gather(pre_values, 'req', axis=0, tiled=True)  27.4 us
    all_gather x1, waiting for transfers between devices, on_device(): lax.all_gather(attn_local, 'req', axis=0, tiled=True)  25.3 us
  transfers between devices with their start and end apart: 6, of which 6 were waited for; matrix products, arithmetic and copies ran while one was open for 3% of the time, Pallas kernels for 0%

profile of v3, /device:TPU:0, one launch (start us, length us, event | category | flops | bytes accessed | tf_op | source)
XLA Modules:
  0.0 366.3 jit_solution(8736294004396407624)
XLA Ops:
  6.6 0.8 select_reduce_fusion
  7.4 10.1 %fusion.45 = (bf16[1024,1,1024]{2,1,0:T(2,128)(2,1)}, bf16[1024,1,1024]{2,1,0:T(2,128)(2,1)}) fusion(bf16[1024,2,1024]{2,1,0:T(2,128)(2,1)} %param.16), kind=kLoop, calls=%fused_computation.106 | loop fusion | bytes 8388608 | tf_op jit(solution)/shard_map/slice | solution.py:201
  17.6 1.6 constant_dynamic-slice_fusion.1
  19.2 2.4 fusion.14
  21.7 0.9 pad_maximum_fusion.2
  22.6 1.6 constant_dynamic-slice_fusion
  24.2 0.7 copy.90
  25.3 0.2 copy.86
  25.5 0.2 copy.85
  25.7 0.3 multiply_cosine_fusion.1
  26.2 0.2 copy.70
  26.4 0.2 copy.71
  26.6 0.2 select_reduce_fusion.4
  26.9 0.9 dynamic-slice_convert_fusion
  28.0 0.3 fusion.47
  28.5 1.1 fusion.22
  29.7 0.3 copy.78
  30.3 0.2 reshape.369
  30.4 0.2 reshape.370
  30.6 0.8 pad_maximum_fusion.1.q_ref
  31.5 19.0 %all-gather.6.cloned.1.call-done.k_ref = bf16[8192,128]{1,0:T(8,128)(2,1)} async-done(((bf16[1024,128]{1,0:T(8,128)(2,1)}), bf16[8192,128]{1,0:T(8,128)(2,1)}) %all-gather.6.cloned.1.call-update) | async-done | bytes 2097168 | tf_op jit(solution)/shard_map/all_gather | solution.py:203
  50.5 27.4 %all-gather.12.cloned.1.call-done = bf16[8192,1,128]{2,0,1:T(8,128)(2,1)} async-done(((bf16[1024,1,128]{2,0,1:T(8,128)(2,1)}), bf16[8192,1,128]{2,0,1:T(8,128)(2,1)}) %all-gather.12.cloned.1.call-update) | async-done | bytes 2097168 | tf_op jit(solution)/shard_map/all_gather | solution.py:204
  77.9 32.4 %shard_map.127 = (f32[1024,1]{1,0:T(8,128)}, f32[1024,1]{1,0:T(8,128)}, f32[1024,128]{1,0:T(8,128)}) custom-call(bf16[1024,128]{1,0:T(8,128)(2,1)} %pad_maximum_fusion.1.q_ref, bf16[8192,128]{1,0:T(8,128)(2,1)} %all-gather.6.cloned.1.call-done.k_ref, bf16[8192,128]{1,0:T(8,128)(2,1)} %bitcast.39), custom_call_target="tpu_custom_call" | custom-call | tf_op jit(solution)/shard_map/pallas_call | solution.py:111
  110.3 1.7 fusion.30
  112.0 1.5 divide_convert_fusion
  113.5 0.9 reshape.351
  114.9 25.3 %all-gather.8.cloned.1.call-done = bf16[2048,512]{1,0:T(8,128)(2,1)} async-done(((bf16[256,512]{1,0:T(8,128)(2,1)}), bf16[2048,512]{1,0:T(8,128)(2,1)}) %all-gather.8.cloned.1.call-update) | async-done | bytes 2097168 | tf_op jit(solution)/shard_map/all_gather | solution.py:217
  140.2 5.8 %gather_fusion = bf16[1024,512]{1,0:T(8,128)(2,1)S(1)} fusion(bf16[2048,512]{1,0:T(8,128)(2,1)} %all-gather.8.cloned.1.call-done, s32[1024]{0:T(1024)S(1)} %broadcast_clamp_fusion), kind=kCustom, calls=%fused_computation | custom fusion | bytes 2101248 | tf_op jit(solution)/shard_map/jit(_take)/gather | solution.py:217
  146.1 2.7 convolution_convert_fusion.3
  148.8 7.0 %all-to-all-start = ((bf16[16,64,1024]{2,1,0:T(8,128)(2,1)}), bf16[16,64,1024]{2,1,0:T(8,128)(2,1)S(1)}, u32[]{:S(2)}, u32[]{:S(2)}) async-start(bf16[16,64,1024]{2,1,0:T(8,128)(2,1)} %bitcast.40), calls=%async_computation | async-start | bytes 4194304 | tf_op jit(solution)/shard_map/all_to_all | solution.py:74
  155.8 33.4 %all-to-all-done = bf16[16,64,1024]{2,1,0:T(8,128)(2,1)S(1)} async-done(((bf16[16,64,1024]{2,1,0:T(8,128)(2,1)}), bf16[16,64,1024]{2,1,0:T(8,128)(2,1)S(1)}, u32[]{:S(2)}, u32[]{:S(2)}) %all-to-all-start) | async-done | bytes 2097184 | tf_op jit(solution)/shard_map/all_to_all | solution.py:74
  189.2 0.4 convert_reduce_fusion.1
  189.6 1.1 add_convert_fusion.2
  190.7 0.3 broadcast_in_dim.25
  190.9 31.4 %all_to_all.15 = bf16[16,64,1024]{2,1,0:T(8,128)(2,1)S(1)} all-to-all(bf16[16,64,1024]{2,1,0:T(8,128)(2,1)S(1)} %broadcast_in_dim.25), channel_id=1, replica_groups=mesh['req'=8,'hid'=16] {'hid'}, dimensions={0} | all-to-all | bytes 4194304 | tf_op jit(solution)/shard_map/all_to_all | solution.py:81
  222.3 5.4 %convolution_convert_fusion = bf16[1024,1792]{1,0:T(8,128)(2,1)} fusion(bf16[1024,1792]{1,0:T(8,128)(2,1)S(1)} %copy-done.5, bf16[1024,1024]{1,0:T(8,128)(2,1)S(1)} %bitcast.35, f32[1024]{0:T(1024)S(1)} %copy-done.7), kind=kOutput, calls=%fused_computation.8 | convolution fusion | flops 3763077120 | bytes 9441280 | tf_op jit(solution)/shard_map/dot_general | solution.py:227
  227.8 5.4 %convolution_convert_fusion.1 = bf16[1024,1792]{1,0:T(8,128)(2,1)} fusion(bf16[1024,1792]{1,0:T(8,128)(2,1)S(1)} %copy-done.6, bf16[1024,1024]{1,0:T(8,128)(2,1)S(1)} %bitcast.36, f32[1024]{0:T(1024)S(1)} %copy-done.7), kind=kOutput, calls=%fused_computation.9 | convolution fusion | flops 3763077120 | bytes 9441280 | tf_op jit(solution)/shard_map/dot_general | solution.py:226
  233.2 6.6 %pad_maximum_fusion = bf16[1024,3584]{1,0:T(8,128)(2,1)} fusion(bf16[1024,1792]{1,0:T(8,128)(2,1)} %convolution_convert_fusion, bf16[1024,1792]{1,0:T(8,128)(2,1)} %convolution_convert_fusion.1), kind=kLoop, calls=%fused_computation.1 | loop fusion | flops 14680064 | bytes 14680064 | tf_op jit(solution)/shard_map/concatenate | solution.py:231
  239.9 0.5 fusion.1
  240.4 12.6 %psum.7 = f32[1024]{0:T(1024)S(1)} all-reduce(f32[1024]{0:T(1024)S(1)} %fusion.1), channel_id=1, replica_groups=mesh['req'=8,'hid'=16] {'req'}, use_global_device_ids=true, to_apply=%region_12.13 | all-reduce | flops 1024 | bytes 8192 | tf_op jit(solution)/shard_map/psum | solution.py:228
  253.1 30.8 %reduce-scatter.2.cloned.1.call-done = bf16[128,3584]{1,0:T(8,128)(2,1)} async-done(((bf16[1024,3584]{1,0:T(8,128)(2,1)}), bf16[128,3584]{1,0:T(8,128)(2,1)}) %reduce-scatter.2.cloned.1.call-update) | async-done | bytes 917520 | tf_op jit(solution)/shard_map/reduce_scatter | solution.py:230
  283.9 1.4 convert_element_type.118
  285.3 1.1 fusion.8
  286.4 29.5 %all-gather.10.cloned.1.call-done = bf16[1024,1792]{1,0:T(8,128)(2,1)} async-done(((bf16[128,1792]{1,0:T(8,128)(2,1)}), bf16[1024,1792]{1,0:T(8,128)(2,1)}) %all-gather.10.cloned.1.call-update) | async-done | bytes 3670032 | tf_op jit(solution)/shard_map/all_gather | solution.py:243
  316.0 7.2 %convolution_convert_fusion.2 = bf16[1024,1024]{1,0:T(8,128)(2,1)S(1)} fusion(bf16[1024,1792]{1,0:T(8,128)(2,1)} %all-gather.10.cloned.1.call-done, bf16[1792,1024]{1,0:T(8,128)(2,1)} %param.25), kind=kOutput, calls=%fused_computation.10 | convolution fusion | flops 3759144960 | bytes 9437184 | tf_op jit(solution)/shard_map/dot_general | solution.py:245
  323.1 35.6 %all_to_all.16 = bf16[16,64,1024]{2,1,0:T(8,128)(2,1)S(1)} all-to-all(bf16[16,64,1024]{2,1,0:T(8,128)(2,1)S(1)} %bitcast.41), channel_id=1, replica_groups=mesh['req'=8,'hid'=16] {'hid'}, dimensions={0} | all-to-all | bytes 4194304 | tf_op jit(solution)/shard_map/all_to_all | solution.py:74
  358.7 0.4 convert_reduce_fusion
  359.1 0.7 add_convert_fusion.1
  (54 shorter events, 2.0 us)
Async XLA Ops:
  6.5 139.6 %copy-start = (bf16[512,1024]{1,0:T(8,128)(2,1)S(1)}, bf16[512,1024]{1,0:T(8,128)(2,1)}, u32[]{:S(2)}) copy-start(bf16[512,1024]{1,0:T(8,128)(2,1)} %param.21) | copy-start | bytes 3145732
  6.5 43.9 %all-gather.6.cloned.1.call-start = ((), (), s32[]{:S(2)}) async-start(), calls=%async_computation.4 | async-start | bytes 2359296 | tf_op jit(solution)/shard_map/all_gather | solution.py:203
  17.5 7.5 %copy-start.2 = (bf16[2,128,512]{2,1,0:T(8,128)(2,1)S(1)}, bf16[2,128,512]{2,1,0:T(8,128)(2,1)}, u32[]{:S(2)}) copy-start(bf16[2,128,512]{2,1,0:T(8,128)(2,1)} %param.13) | copy-start | bytes 786436
  22.5 55.3 %all-gather.12.cloned.1.call-start = ((), (), s32[]{:S(2)}) async-start(), calls=%async_computation.8 | async-start | bytes 2359296 | tf_op jit(solution)/shard_map/all_gather | solution.py:204
  24.2 2.4 copy-start.3
  24.2 2.4 copy-start.4
  25.0 115.3 %all-gather.8.cloned.1.call-start = ((), (), s32[]{:S(2)}) async-start(), calls=%async_computation.5 | async-start | bytes 2359296 | tf_op jit(solution)/shard_map/all_gather | solution.py:217
  148.8 40.4 %all-to-all-start = ((bf16[16,64,1024]{2,1,0:T(8,128)(2,1)}), bf16[16,64,1024]{2,1,0:T(8,128)(2,1)S(1)}, u32[]{:S(2)}, u32[]{:S(2)}) async-start(bf16[16,64,1024]{2,1,0:T(8,128)(2,1)} %bitcast.40), calls=%async_computation | async-start | bytes 4194304 | tf_op jit(solution)/shard_map/all_to_all | solution.py:74
  155.8 128.2 %reduce-scatter.2.cloned.1.call-start = ((), (), s32[]{:S(2)}) async-start(), calls=%async_computation.6 | async-start | bytes 8257536 | tf_op jit(solution)/shard_map/reduce_scatter | solution.py:230
  189.6 32.8 %copy-start.5 = (bf16[1024,1792]{1,0:T(8,128)(2,1)S(1)}, bf16[1024,1792]{1,0:T(8,128)(2,1)}, u32[]{:S(2)}) copy-start(bf16[1024,1792]{1,0:T(8,128)(2,1)} %param.24) | copy-start | bytes 11010052
  189.6 32.7 %copy-start.7 = (f32[1024]{0:T(1024)S(1)}, f32[1024]{0:T(1024)}, u32[]{:S(2)}) copy-start(f32[1024]{0:T(1024)} %param.22) | copy-start | bytes 12292
  222.3 5.4 %copy-start.6 = (bf16[1024,1792]{1,0:T(8,128)(2,1)S(1)}, bf16[1024,1792]{1,0:T(8,128)(2,1)}, u32[]{:S(2)}) copy-start(bf16[1024,1792]{1,0:T(8,128)(2,1)} %param.23) | copy-start | bytes 11010052
  239.9 76.1 %all-gather.10.cloned.1.call-start = ((), (), s32[]{:S(2)}) async-start(), calls=%async_computation.7 | async-start | bytes 4128768 | tf_op jit(solution)/shard_map/all_gather | solution.py:243
  316.0 43.8 %copy-start.1 = (bf16[512,1024]{1,0:T(8,128)(2,1)S(1)}, bf16[512,1024]{1,0:T(8,128)(2,1)}, u32[]{:S(2)}) copy-start(bf16[512,1024]{1,0:T(8,128)(2,1)} %param.21) | copy-start | bytes 3145732
Sparse Core Ops, SparseCore 0:
  22.7 27.7 all-gather.5
  52.2 25.6 all-gather.11
  114.5 25.6 all-gather.7
  240.0 43.9 reduce-scatter.1
  286.6 29.3 all-gather.9

commit v4 on v2

--- a/solution.py
+++ b/solution.py
@@ -146,11 +146,12 @@
     ).astype(jnp.int32)
     logical_block = jnp.sum(block_match * prefix_block[None, :], axis=1)
     pre_pos = (logical_block * PBLK + row_ids % PBLK).astype(jnp.float32)
-    pre_keys = rotate(
-        lax.dynamic_slice_in_dim(prefix_cache[:, 0], kv_head * HD, HD, 1).astype(jnp.float32),
-        pre_pos,
-    ).astype(jnp.bfloat16)
-    pre_values = lax.dynamic_slice_in_dim(prefix_cache[:, 1], kv_head * HD, HD, 1)
+    key_block = lax.dynamic_slice(prefix_cache, (0, 0, kv_head * HD), (local_prefix, 1, HD))
+    pre_keys = rotate(key_block.reshape(local_prefix, HD).astype(jnp.float32), pre_pos).astype(
+        jnp.bfloat16
+    )
+    value_block = lax.dynamic_slice(prefix_cache, (0, 1, kv_head * HD), (local_prefix, 1, HD))
+    pre_values = value_block.reshape(local_prefix, HD)
     query_flat = query_rot.reshape(all_rows, HD)
     run_max = jnp.full((all_rows,), MASKED, jnp.float32)
     keys_piece = lax.all_gather(pre_keys, "req", axis=0, tiled=True)

time: 346 us -> 336 us (0.971)
  local copies, waits for them, and re-layouts: 23.6 us -> 12.7 us
    slice x1 -> x0, local copies, waits for them, and re-layouts: 10.2 us -> none  [on_device(): prefix_cache[:, 0]]
where the time goes in v4:
time: 336 us; the launch traced here: 335 us
  waiting for transfers between devices  140 us (42%)
  blocking collectives  79.4 us (24%)
  matrix products  51.2 us (15%)
  other arithmetic  30.8 us (9%)
  between operations  13.5 us (4%)
  local copies, waits for them, and re-layouts  12.7 us (4%)
  starting transfers between devices  7.33 us (2%)
    all_to_all x1, blocking collectives, exchange_sum(): lax.all_to_all(values.reshape(count, values.shape[0] // count, values.sha...  35.6 us
    all_to_all x1, waiting for transfers between devices, exchange_sum(): lax.all_to_all(values.reshape(count, values.shape[0] // count, values.sha...  33.4 us
    all_to_all x1, blocking collectives, exchange_gather(): lax.all_to_all(jnp.broadcast_to(values[None], (count,) + values.shape), a...  31.2 us
    reduce_scatter x1, waiting for transfers between devices, on_device(): lax.psum_scatter(jnp.concatenate([gate_part.astype(jnp.bfloat16), up_part...  30.8 us
    all_gather x1, waiting for transfers between devices, on_device(): hidden_all = lax.all_gather(hidden, 'req', axis=0, tiled=True)  29.5 us
    all_gather x1, waiting for transfers between devices, on_device(): lax.all_gather(attn_local, 'req', axis=0, tiled=True)  25.3 us
    all_gather x1, waiting for transfers between devices, on_device(): keys_piece = lax.all_gather(pre_keys, 'req', axis=0, tiled=True)  21.3 us
    dot_general x1, matrix products, on_device(): jnp.einsum('rd,pd->rp', query_flat, keys_piece, preferred_element_type=jn...  15.1 us
  transfers between devices with their start and end apart: 6, of which 5 were waited for; matrix products, arithmetic and copies ran while one was open for 11% of the time, Pallas kernels for 0%

profile of v4, /device:TPU:0, one launch (start us, length us, event | category | flops | bytes accessed | tf_op | source)
XLA Modules:
  0.0 335.4 jit_solution(10672512226343056291)
XLA Ops:
  6.6 2.5 constant_dynamic-slice_fusion.1
  9.1 0.4 copy.66
  9.7 1.2 fusion.42
  10.8 0.7 pad_maximum_fusion.1
  11.6 0.7 copy.67
  12.4 0.2 all-gather.8.cloned.1.call-start
  12.7 0.3 multiply_cosine_fusion.1
  13.0 0.2 copy.50
  13.2 0.2 copy.64
  13.4 0.2 copy.65
  13.6 0.1 subtract_convert_fusion
  13.8 0.2 copy.53
  14.0 0.2 copy.54
  14.2 0.9 dynamic-slice_convert_fusion
  15.2 0.2 select_reduce_fusion.4
  15.7 0.3 fusion.76
  16.0 0.1 copy.57
  16.2 1.1 fusion.45
  17.4 0.1 copy.60
  17.8 0.3 copy.59
  18.1 21.3 %all-gather.6.cloned.1.call-done = bf16[8192,128]{0,1:T(8,128)(2,1)} async-done(((bf16[1024,128]{0,1:T(8,128)(2,1)}), bf16[8192,128]{0,1:T(8,128)(2,1)}) %all-gather.6.cloned.1.call-update) | async-done | bytes 2097168 | tf_op jit(solution)/shard_map/all_gather | solution.py:157
  39.4 15.1 %multiply_reduce_fusion = (f32[1024]{0:T(1024)S(1)}, f32[1024,8192]{1,0:T(8,128)}) fusion(bf16[8192,128]{0,1:T(8,128)(2,1)} %all-gather.6.cloned.1.call-done, bf16[1024,64]{1,0:T(8,128)(2,1)S(1)} %bitcast.51, bf16[1024,64]{1,0:T(8,128)(2,1)S(1)} %bitcast.50), kind=kOutput, calls=%fused_computation.2 | convolution fusion | flops 2164784128 | bytes 35917824 | tf_op jit(solution)/shard_map/rd,pd->rp/dot_general | solution.py:160
  54.5 14.2 %fusion = f32[1024]{0:T(1024)S(1)} fusion(f32[1024,8192]{1,0:T(8,128)} %get-tuple-element.25, f32[1024]{0:T(1024)S(1)} %broadcast_maximum_fusion), kind=kLoop, calls=%fused_computation.3 | loop fusion | flops 25164800 | bytes 33562624 | tf_op jit(solution)/shard_map/reduce_sum | solution.py:164
  68.8 14.0 %fusion.25 = bf16[1024,128]{1,0:T(8,128)(2,1)S(1)} fusion(bf16[8192,1,128]{2,0,1:T(8,128)(2,1)} %all-gather.12.cloned.1.call-done, f32[1024,8192]{1,0:T(8,128)} %get-tuple-element.25, f32[1024]{0:T(1024)S(1)} %broadcast_maximum_fusion, f32[1024,128]{1,0:T(8,128)S(1)} %bitcast.52, f32[1024]{0:T(1024)S(1)} %get-tuple-element.9, ...), kind=kOutput, calls=%fused_computation.23 | convolution fusion | flops 2173304832 | bytes 36454400 | tf_op jit(solution)/shard_map/dot_general | solution.py:165
  82.8 0.9 reshape.386
  83.8 0.1 reduce
  84.2 25.3 %all-gather.8.cloned.1.call-done = bf16[2048,512]{1,0:T(8,128)(2,1)} async-done(((bf16[256,512]{1,0:T(8,128)(2,1)}), bf16[2048,512]{1,0:T(8,128)(2,1)}) %all-gather.8.cloned.1.call-update) | async-done | bytes 2097168 | tf_op jit(solution)/shard_map/all_gather | solution.py:177
  109.5 5.8 %gather_fusion = bf16[1024,512]{1,0:T(8,128)(2,1)S(1)} fusion(bf16[2048,512]{1,0:T(8,128)(2,1)} %all-gather.8.cloned.1.call-done, s32[1024]{0:T(1024)S(1)} %broadcast_clamp_fusion), kind=kCustom, calls=%fused_computation | custom fusion | bytes 2101248 | tf_op jit(solution)/shard_map/jit(_take)/gather | solution.py:177
  115.3 2.7 convolution_convert_fusion.3
  118.0 7.0 %all-to-all-start = ((bf16[16,64,1024]{2,1,0:T(8,128)(2,1)}), bf16[16,64,1024]{2,1,0:T(8,128)(2,1)S(1)}, u32[]{:S(2)}, u32[]{:S(2)}) async-start(bf16[16,64,1024]{2,1,0:T(8,128)(2,1)} %bitcast.48), calls=%async_computation | async-start | bytes 4194304 | tf_op jit(solution)/shard_map/all_to_all | solution.py:72
  125.0 33.4 %all-to-all-done = bf16[16,64,1024]{2,1,0:T(8,128)(2,1)S(1)} async-done(((bf16[16,64,1024]{2,1,0:T(8,128)(2,1)}), bf16[16,64,1024]{2,1,0:T(8,128)(2,1)S(1)}, u32[]{:S(2)}, u32[]{:S(2)}) %all-to-all-start) | async-done | bytes 2097184 | tf_op jit(solution)/shard_map/all_to_all | solution.py:72
  158.4 0.4 convert_reduce_fusion.1
  158.8 1.1 add_convert_fusion.2
  159.9 0.3 broadcast_in_dim.28
  160.2 31.2 %all_to_all.15 = bf16[16,64,1024]{2,1,0:T(8,128)(2,1)S(1)} all-to-all(bf16[16,64,1024]{2,1,0:T(8,128)(2,1)S(1)} %broadcast_in_dim.28), channel_id=1, replica_groups=mesh['req'=8,'hid'=16] {'hid'}, dimensions={0} | all-to-all | bytes 4194304 | tf_op jit(solution)/shard_map/all_to_all | solution.py:79
  191.4 5.4 %convolution_convert_fusion = bf16[1024,1792]{1,0:T(8,128)(2,1)} fusion(bf16[1024,1792]{1,0:T(8,128)(2,1)S(1)} %copy-done.6, bf16[1024,1024]{1,0:T(8,128)(2,1)S(1)} %bitcast.44, f32[1024]{0:T(1024)S(1)} %copy-done.8), kind=kOutput, calls=%fused_computation.13 | convolution fusion | flops 3763077120 | bytes 9441280 | tf_op jit(solution)/shard_map/dot_general | solution.py:187
  196.8 5.4 %convolution_convert_fusion.1 = bf16[1024,1792]{1,0:T(8,128)(2,1)} fusion(bf16[1024,1792]{1,0:T(8,128)(2,1)S(1)} %copy-done.7, bf16[1024,1024]{1,0:T(8,128)(2,1)S(1)} %bitcast.45, f32[1024]{0:T(1024)S(1)} %copy-done.8), kind=kOutput, calls=%fused_computation.14 | convolution fusion | flops 3763077120 | bytes 9441280 | tf_op jit(solution)/shard_map/dot_general | solution.py:186
  202.2 6.6 %pad_maximum_fusion = bf16[1024,3584]{1,0:T(8,128)(2,1)} fusion(bf16[1024,1792]{1,0:T(8,128)(2,1)} %convolution_convert_fusion, bf16[1024,1792]{1,0:T(8,128)(2,1)} %convolution_convert_fusion.1), kind=kLoop, calls=%fused_computation.6 | loop fusion | flops 14680064 | bytes 14680064 | tf_op jit(solution)/shard_map/concatenate | solution.py:191
  209.0 0.5 fusion.5
  209.4 12.6 %psum.7 = f32[1024]{0:T(1024)S(1)} all-reduce(f32[1024]{0:T(1024)S(1)} %fusion.5), channel_id=1, replica_groups=mesh['req'=8,'hid'=16] {'req'}, use_global_device_ids=true, to_apply=%region_14.15 | all-reduce | flops 1024 | bytes 8192 | tf_op jit(solution)/shard_map/psum | solution.py:188
  222.2 30.8 %reduce-scatter.2.cloned.1.call-done = bf16[128,3584]{1,0:T(8,128)(2,1)} async-done(((bf16[1024,3584]{1,0:T(8,128)(2,1)}), bf16[128,3584]{1,0:T(8,128)(2,1)}) %reduce-scatter.2.cloned.1.call-update) | async-done | bytes 917520 | tf_op jit(solution)/shard_map/reduce_scatter | solution.py:190
  253.0 1.4 convert_element_type.122
  254.4 1.1 fusion.33
  255.5 29.5 %all-gather.10.cloned.1.call-done = bf16[1024,1792]{1,0:T(8,128)(2,1)} async-done(((bf16[128,1792]{1,0:T(8,128)(2,1)}), bf16[1024,1792]{1,0:T(8,128)(2,1)}) %all-gather.10.cloned.1.call-update) | async-done | bytes 3670032 | tf_op jit(solution)/shard_map/all_gather | solution.py:203
  285.0 7.2 %convolution_convert_fusion.2 = bf16[1024,1024]{1,0:T(8,128)(2,1)S(1)} fusion(bf16[1024,1792]{1,0:T(8,128)(2,1)} %all-gather.10.cloned.1.call-done, bf16[1792,1024]{1,0:T(8,128)(2,1)} %param.25), kind=kOutput, calls=%fused_computation.16 | convolution fusion | flops 3759144960 | bytes 9437184 | tf_op jit(solution)/shard_map/dot_general | solution.py:205
  292.2 35.6 %all_to_all.16 = bf16[16,64,1024]{2,1,0:T(8,128)(2,1)S(1)} all-to-all(bf16[16,64,1024]{2,1,0:T(8,128)(2,1)S(1)} %bitcast.49), channel_id=1, replica_groups=mesh['req'=8,'hid'=16] {'hid'}, dimensions={0} | all-to-all | bytes 4194304 | tf_op jit(solution)/shard_map/all_to_all | solution.py:72
  327.8 0.4 convert_reduce_fusion
  328.2 0.7 add_convert_fusion.1
  (56 shorter events, 1.6 us)
Async XLA Ops:
  6.5 108.8 %copy-start = (bf16[512,1024]{1,0:T(8,128)(2,1)S(1)}, bf16[512,1024]{1,0:T(8,128)(2,1)}, u32[]{:S(2)}) copy-start(bf16[512,1024]{1,0:T(8,128)(2,1)} %param.21) | copy-start | bytes 3145732
  6.5 3.0 copy-start.4
  6.5 6.4 %copy-start.2 = (bf16[2,128,512]{2,1,0:T(8,128)(2,1)S(1)}, bf16[2,128,512]{2,1,0:T(8,128)(2,1)}, u32[]{:S(2)}) copy-start(bf16[2,128,512]{2,1,0:T(8,128)(2,1)} %param.13) | copy-start | bytes 786436
  6.5 32.9 %all-gather.6.cloned.1.call-start = ((), (), s32[]{:S(2)}) async-start(), calls=%async_computation.4 | async-start | bytes 2359296 | tf_op jit(solution)/shard_map/all_gather | solution.py:157
  11.6 57.2 %all-gather.12.cloned.1.call-start = ((), (), s32[]{:S(2)}) async-start(), calls=%async_computation.8 | async-start | bytes 2359296 | tf_op jit(solution)/shard_map/all_gather | solution.py:158
  12.4 2.8 copy-start.3
  12.4 2.8 copy-start.5
  12.4 97.1 %all-gather.8.cloned.1.call-start = ((), (), s32[]{:S(2)}) async-start(), calls=%async_computation.5 | async-start | bytes 2359296 | tf_op jit(solution)/shard_map/all_gather | solution.py:177
  118.0 40.4 %all-to-all-start = ((bf16[16,64,1024]{2,1,0:T(8,128)(2,1)}), bf16[16,64,1024]{2,1,0:T(8,128)(2,1)S(1)}, u32[]{:S(2)}, u32[]{:S(2)}) async-start(bf16[16,64,1024]{2,1,0:T(8,128)(2,1)} %bitcast.48), calls=%async_computation | async-start | bytes 4194304 | tf_op jit(solution)/shard_map/all_to_all | solution.py:72
  125.0 128.0 %reduce-scatter.2.cloned.1.call-start = ((), (), s32[]{:S(2)}) async-start(), calls=%async_computation.6 | async-start | bytes 8257536 | tf_op jit(solution)/shard_map/reduce_scatter | solution.py:190
  158.8 32.6 %copy-start.6 = (bf16[1024,1792]{1,0:T(8,128)(2,1)S(1)}, bf16[1024,1792]{1,0:T(8,128)(2,1)}, u32[]{:S(2)}) copy-start(bf16[1024,1792]{1,0:T(8,128)(2,1)} %param.24) | copy-start | bytes 11010052
  158.8 32.6 %copy-start.8 = (f32[1024]{0:T(1024)S(1)}, f32[1024]{0:T(1024)}, u32[]{:S(2)}) copy-start(f32[1024]{0:T(1024)} %param.22) | copy-start | bytes 12292
  191.4 5.4 %copy-start.7 = (bf16[1024,1792]{1,0:T(8,128)(2,1)S(1)}, bf16[1024,1792]{1,0:T(8,128)(2,1)}, u32[]{:S(2)}) copy-start(bf16[1024,1792]{1,0:T(8,128)(2,1)} %param.23) | copy-start | bytes 11010052
  208.9 76.1 %all-gather.10.cloned.1.call-start = ((), (), s32[]{:S(2)}) async-start(), calls=%async_computation.7 | async-start | bytes 4128768 | tf_op jit(solution)/shard_map/all_gather | solution.py:203
  285.0 43.8 %copy-start.1 = (bf16[512,1024]{1,0:T(8,128)(2,1)S(1)}, bf16[512,1024]{1,0:T(8,128)(2,1)}, u32[]{:S(2)}) copy-start(bf16[512,1024]{1,0:T(8,128)(2,1)} %param.21) | copy-start | bytes 3145732
Sparse Core Ops, SparseCore 0:
  11.7 27.6 all-gather.5
  41.1 25.5 all-gather.11
  83.8 25.6 all-gather.7
  209.0 43.9 reduce-scatter.1
  255.6 29.3 all-gather.9

commit v5 on v4

--- a/solution.py
+++ b/solution.py
@@ -175,36 +175,62 @@
     own_rows = tokens // hid_count
     source = token_source(suffix_len, slot_request, tokens, maxlen)
     token_rows = jnp.take(lax.all_gather(attn_local, "req", axis=0, tiled=True), source, axis=0)
-    projected = jnp.dot(token_rows, out_weight, preferred_element_type=jnp.float32)
-    summed = exchange_sum(projected.astype(jnp.bfloat16), "hid", hid_count)
-    residual_own = lax.dynamic_slice_in_dim(residual, hid_index * own_rows, own_rows, 0)
-    resid_own = (residual_own.astype(jnp.float32) + summed).astype(jnp.bfloat16)
-    resid_all = exchange_gather(resid_own, "hid", hid_count)
-    resid_f = lax.optimization_barrier(resid_all).astype(jnp.float32)
-    squares = jnp.sum(resid_f * resid_f, axis=1)
-    scaled = (resid_f * post_gain[None, :]).astype(jnp.bfloat16)
-    gate_part = jnp.dot(scaled, gate_weight, preferred_element_type=jnp.float32)
-    up_part = jnp.dot(scaled, up_weight, preferred_element_type=jnp.float32)
-    square_all = lax.psum(squares, "req")
-    ff_cols = gate_part.shape[1]
-    both_sum = lax.psum_scatter(
-        jnp.concatenate([gate_part.astype(jnp.bfloat16), up_part.astype(jnp.bfloat16)], axis=1),
-        "req",
-        scatter_dimension=0,
-        tiled=True,
-    ).astype(jnp.float32)
-    gate_sum, up_sum = both_sum[:, :ff_cols], both_sum[:, ff_cols:]
-    row_count = tokens // req_count
-    square_sum = lax.dynamic_slice_in_dim(square_all, req_index * row_count, row_count, 0)
-    inv_rms = lax.rsqrt(square_sum / D + EPSILON)
-    hidden = (jax.nn.silu(gate_sum * inv_rms[:, None]) * (up_sum * inv_rms[:, None])).astype(
+    projected = jnp.dot(token_rows, out_weight, preferred_element_type=jnp.float32).astype(
         jnp.bfloat16
     )
-    hidden_all = lax.all_gather(hidden, "req", axis=0, tiled=True)
-    mixed_rows = exchange_sum(
-        jnp.dot(hidden_all, down_weight, preferred_element_type=jnp.float32).astype(jnp.bfloat16),
-        "hid",
-        hid_count,
+    halves = 2
+    half = tokens // halves
+    piece = half // hid_count
+    row_count = half // req_count
+    ff_cols = gate_weight.shape[1]
+    resid_halves, square_halves, both_halves = [], [], []
+    for c in range(halves):
+        summed = exchange_sum(projected[c * half : (c + 1) * half], "hid", hid_count)
+        residual_piece = lax.dynamic_slice_in_dim(residual, c * half + hid_index * piece, piece, 0)
+        resid_piece = (residual_piece.astype(jnp.float32) + summed).astype(jnp.bfloat16)
+        resid_half = exchange_gather(resid_piece, "hid", hid_count)
+        resid_halves.append(resid_half)
+        resid_f = lax.optimization_barrier(resid_half).astype(jnp.float32)
+        square_halves.append(jnp.sum(resid_f * resid_f, axis=1))
+        scaled = (resid_f * post_gain[None, :]).astype(jnp.bfloat16)
+        gate_part = jnp.dot(scaled, gate_weight, preferred_element_type=jnp.float32)
+        up_part = jnp.dot(scaled, up_weight, preferred_element_type=jnp.float32)
+        both_halves.append(
+            lax.psum_scatter(
+                jnp.concatenate(
+                    [gate_part.astype(jnp.bfloat16), up_part.astype(jnp.bfloat16)], axis=1
+                ),
+                "req",
+                scatter_dimension=0,
+                tiled=True,
+            ).astype(jnp.float32)
+        )
+    square_all = lax.psum(jnp.concatenate(square_halves), "req")
+    hidden_halves = []
+    for c in range(halves):
+        square_sum = lax.dynamic_slice_in_dim(
+            square_all, c * half + req_index * row_count, row_count, 0
+        )
+        inv_rms = lax.rsqrt(square_sum / D + EPSILON)
+        gate_sum, up_sum = both_halves[c][:, :ff_cols], both_halves[c][:, ff_cols:]
+        hidden_halves.append(
+            (jax.nn.silu(gate_sum * inv_rms[:, None]) * (up_sum * inv_rms[:, None])).astype(
+                jnp.bfloat16
+            )
+        )
+    hidden_all = lax.all_gather(jnp.concatenate(hidden_halves), "req", axis=0, tiled=True)
+    down = jnp.dot(hidden_all, down_weight, preferred_element_type=jnp.float32).astype(
+        jnp.bfloat16
+    )
+    width = down.shape[1]
+    down = (
+        down.reshape(req_count, halves, row_count, width)
+        .transpose(1, 0, 2, 3)
+        .reshape(tokens, width)
+    )
+    mixed_rows = exchange_sum(down, "hid", hid_count)
+    resid_own = lax.dynamic_slice_in_dim(
+        jnp.concatenate(resid_halves), hid_index * own_rows, own_rows, 0
     )
     return (resid_own.astype(jnp.float32) + mixed_rows).astype(jnp.bfloat16)
 

time: 336 us -> 353 us (1.051)
  waiting for transfers between devices: 140 us -> 155 us
  starting transfers between devices: 7.33 us -> 11.6 us
  blocking collectives: 79.4 us -> 75.5 us
    all_to_all x1 -> x2, waiting for transfers between devices: 33.4 us -> 49.7 us  [exchange_sum(): lax.all_to_all(values.reshape(count, values.shape[0] // count, values.sha...]
    all_to_all x1, blocking collectives: 35.6 us -> 24.3 us  [exchange_sum(): lax.all_to_all(values.reshape(count, values.shape[0] // count, values.sha...]
    all_to_all x1 -> x2, blocking collectives: 31.2 us -> 38.8 us  [exchange_gather(): lax.all_to_all(jnp.broadcast_to(values[None], (count,) + values.shape), a...]
    all_to_all x1 -> x2, starting transfers between devices: 6.98 us -> 10.9 us  [exchange_sum(): lax.all_to_all(values.reshape(count, values.shape[0] // count, values.sha...]
    reduce_scatter x1 -> x2, waiting for transfers between devices: 30.8 us -> 29.6 us  [on_device(): lax.psum_scatter(jnp.concatenate([gate_part.astype(jnp.bfloat16), up_part...]
  transfers between devices with their start and end apart: 6 -> 8, of which waited for: 5 -> 6; matrix products, arithmetic and copies ran while one was open for 11% -> 13% of each run, Pallas kernels for 0% -> 0%
where the time goes in v5:
time: 353 us; the launch traced here: 352 us
  waiting for transfers between devices  155 us (44%)
  blocking collectives  75.5 us (21%)
  matrix products  49.6 us (14%)
  other arithmetic  31 us (9%)
  local copies, waits for them, and re-layouts  15.4 us (4%)
  between operations  13.9 us (4%)
  starting transfers between devices  11.6 us (3%)
    all_to_all x2, waiting for transfers between devices, exchange_sum(): lax.all_to_all(values.reshape(count, values.shape[0] // count, values.sha...  49.7 us
    all_to_all x2, blocking collectives, exchange_gather(): lax.all_to_all(jnp.broadcast_to(values[None], (count,) + values.shape), a...  38.8 us
    reduce_scatter x2, waiting for transfers between devices, on_device(): lax.psum_scatter(jnp.concatenate([gate_part.astype(jnp.bfloat16), up_part...  29.6 us
    all_gather x1, waiting for transfers between devices, on_device(): lax.all_gather(jnp.concatenate(hidden_halves), 'req', axis=0, tiled=True)  28.8 us
    all_gather x1, waiting for transfers between devices, on_device(): lax.all_gather(attn_local, 'req', axis=0, tiled=True)  25.3 us
    all_to_all x1, blocking collectives, exchange_sum(): lax.all_to_all(values.reshape(count, values.shape[0] // count, values.sha...  24.3 us
    all_gather x1, waiting for transfers between devices, on_device(): keys_piece = lax.all_gather(pre_keys, 'req', axis=0, tiled=True)  21.3 us
    dot_general x1, matrix products, on_device(): jnp.einsum('rd,pd->rp', query_flat, keys_piece, preferred_element_type=jn...  15.1 us
  transfers between devices with their start and end apart: 8, of which 6 were waited for; matrix products, arithmetic and copies ran while one was open for 13% of the time, Pallas kernels for 0%

profile of v5, /device:TPU:0, one launch (start us, length us, event | category | flops | bytes accessed | tf_op | source)
XLA Modules:
  0.0 351.7 jit_solution(17145672878683074326)
XLA Ops:
  6.6 2.5 constant_dynamic-slice_fusion.1
  9.1 0.4 copy.70
  9.7 1.2 fusion.48
  10.8 0.7 pad_maximum_fusion.3
  11.6 0.7 copy.71
  12.4 0.2 all-gather.8.cloned.1.call-start
  12.7 0.3 multiply_cosine_fusion.1
  14.2 0.9 dynamic-slice_convert_fusion
  15.7 0.3 fusion.84
  16.2 1.1 fusion.51
  17.8 0.3 copy.62
  18.1 21.3 %all-gather.6.cloned.1.call-done = bf16[8192,128]{0,1:T(8,128)(2,1)} async-done(((bf16[1024,128]{0,1:T(8,128)(2,1)}), bf16[8192,128]{0,1:T(8,128)(2,1)}) %all-gather.6.cloned.1.call-update) | async-done | bytes 2097168 | tf_op jit(solution)/shard_map/all_gather | solution.py:157
  39.4 15.1 %multiply_reduce_fusion = (f32[1024]{0:T(1024)S(1)}, f32[1024,8192]{1,0:T(8,128)}) fusion(bf16[8192,128]{0,1:T(8,128)(2,1)} %all-gather.6.cloned.1.call-done, bf16[1024,64]{1,0:T(8,128)(2,1)S(1)} %bitcast.64, bf16[1024,64]{1,0:T(8,128)(2,1)S(1)} %bitcast.63), kind=kOutput, calls=%fused_computation.2 | convolution fusion | flops 2164784128 | bytes 35917824 | tf_op jit(solution)/shard_map/rd,pd->rp/dot_general | solution.py:160
  54.5 14.2 %fusion = f32[1024]{0:T(1024)S(1)} fusion(f32[1024,8192]{1,0:T(8,128)} %get-tuple-element.31, f32[1024]{0:T(1024)S(1)} %broadcast_maximum_fusion), kind=kLoop, calls=%fused_computation.3 | loop fusion | flops 25164800 | bytes 33562624 | tf_op jit(solution)/shard_map/reduce_sum | solution.py:164
  68.8 14.0 %fusion.25 = bf16[1024,128]{1,0:T(8,128)(2,1)S(1)} fusion(bf16[8192,1,128]{2,0,1:T(8,128)(2,1)} %all-gather.12.cloned.1.call-done, f32[1024,8192]{1,0:T(8,128)} %get-tuple-element.31, f32[1024]{0:T(1024)S(1)} %broadcast_maximum_fusion, f32[1024,128]{1,0:T(8,128)S(1)} %bitcast.65, f32[1024]{0:T(1024)S(1)} %get-tuple-element.9, ...), kind=kOutput, calls=%fused_computation.33 | convolution fusion | flops 2173304832 | bytes 36454400 | tf_op jit(solution)/shard_map/dot_general | solution.py:165
  82.8 0.9 reshape.394
  84.2 25.3 %all-gather.8.cloned.1.call-done = bf16[2048,512]{1,0:T(8,128)(2,1)} async-done(((bf16[256,512]{1,0:T(8,128)(2,1)}), bf16[2048,512]{1,0:T(8,128)(2,1)}) %all-gather.8.cloned.1.call-update) | async-done | bytes 2097168 | tf_op jit(solution)/shard_map/all_gather | solution.py:177
  109.5 5.8 %gather_fusion = bf16[1024,512]{1,0:T(8,128)(2,1)S(1)} fusion(bf16[2048,512]{1,0:T(8,128)(2,1)} %all-gather.8.cloned.1.call-done, s32[1024]{0:T(1024)S(1)} %broadcast_clamp_fusion), kind=kCustom, calls=%fused_computation | custom fusion | bytes 2101248 | tf_op jit(solution)/shard_map/jit(_take)/gather | solution.py:177
  115.3 1.3 convolution_convert_fusion.5
  116.6 1.2 fusion.82
  117.8 24.3 %all_to_all.25 = bf16[16,32,1024]{2,1,0:T(8,128)(2,1)S(1)} all-to-all(bf16[16,32,1024]{2,1,0:T(8,128)(2,1)S(1)} %bitcast.60), channel_id=1, replica_groups=mesh['req'=8,'hid'=16] {'hid'}, dimensions={0} | all-to-all | bytes 2097152 | tf_op jit(solution)/shard_map/all_to_all | solution.py:72
  142.1 3.8 %all-to-all-start = ((bf16[16,32,1024]{2,1,0:T(8,128)(2,1)}), bf16[16,32,1024]{2,1,0:T(8,128)(2,1)S(1)}, u32[]{:S(2)}, u32[]{:S(2)}) async-start(bf16[16,32,1024]{2,1,0:T(8,128)(2,1)} %bitcast.16), calls=%async_computation | async-start | bytes 2097152 | tf_op jit(solution)/shard_map/all_to_all | solution.py:72
  145.9 0.3 reduce-scatter.3.cloned.1.call-start
  146.4 16.2 %all-to-all-done = bf16[16,32,1024]{2,1,0:T(8,128)(2,1)S(1)} async-done(((bf16[16,32,1024]{2,1,0:T(8,128)(2,1)}), bf16[16,32,1024]{2,1,0:T(8,128)(2,1)S(1)}, u32[]{:S(2)}, u32[]{:S(2)}) %all-to-all-start) | async-done | bytes 1048608 | tf_op jit(solution)/shard_map/all_to_all | solution.py:72
  162.8 1.1 add_convert_fusion.3
  164.0 19.6 %all_to_all.26 = bf16[16,32,1024]{2,1,0:T(8,128)(2,1)S(1)} all-to-all(bf16[16,32,1024]{2,1,0:T(8,128)(2,1)S(1)} %broadcast_in_dim.30), channel_id=1, replica_groups=mesh['req'=8,'hid'=16] {'hid'}, dimensions={0} | all-to-all | bytes 2097152 | tf_op jit(solution)/shard_map/all_to_all | solution.py:79
  183.6 2.1 convolution_convert_fusion.2
  185.7 2.1 convolution_convert_fusion.3
  187.8 2.1 pad_maximum_fusion
  190.1 19.2 %all_to_all.27 = bf16[16,32,1024]{2,1,0:T(8,128)(2,1)S(1)} all-to-all(bf16[16,32,1024]{2,1,0:T(8,128)(2,1)S(1)} %broadcast_in_dim.31), channel_id=1, replica_groups=mesh['req'=8,'hid'=16] {'hid'}, dimensions={0} | all-to-all | bytes 2097152 | tf_op jit(solution)/shard_map/all_to_all | solution.py:79
  209.3 4.3 %convolution_convert_fusion = bf16[512,1792]{1,0:T(8,128)(2,1)S(1)} fusion(bf16[1024,1792]{1,0:T(8,128)(2,1)} %param.24, bf16[512,1024]{1,0:T(8,128)(2,1)S(1)} %bitcast.55, f32[1024]{0:T(1024)S(1)} %copy-done.9), kind=kOutput, calls=%fused_computation.9 | convolution fusion | flops 1881538560 | bytes 6557696 | tf_op jit(solution)/shard_map/dot_general | solution.py:197
  213.6 2.1 convolution_convert_fusion.1
  215.8 2.1 pad_maximum_fusion.1
  217.9 0.3 fusion.5
  218.2 0.3 fusion.6
  218.5 12.4 %psum.7 = f32[1024]{0:T(1024)S(1)} all-reduce(f32[1024]{0:T(1024)S(1)} %pad_maximum_fusion.4), channel_id=1, replica_groups=mesh['req'=8,'hid'=16] {'req'}, use_global_device_ids=true, to_apply=%region_16.17 | all-reduce | flops 1024 | bytes 8192 | tf_op jit(solution)/shard_map/psum | solution.py:208
  231.0 1.1 convert_element_type.152
  232.1 0.2 fusion.42
  232.3 29.6 %reduce-scatter.5.cloned.1.call-done = bf16[64,3584]{1,0:T(8,128)(2,1)} async-done(((bf16[512,3584]{1,0:T(8,128)(2,1)}), bf16[64,3584]{1,0:T(8,128)(2,1)}) %reduce-scatter.5.cloned.1.call-update) | async-done | bytes 458768 | tf_op jit(solution)/shard_map/reduce_scatter | solution.py:199
  261.9 1.1 convert_element_type.158
  263.2 0.8 pad_maximum_fusion.2
  264.0 28.8 %all-gather.10.cloned.1.call-done = bf16[1024,1792]{1,0:T(8,128)(2,1)} async-done(((bf16[128,1792]{1,0:T(8,128)(2,1)}), bf16[1024,1792]{1,0:T(8,128)(2,1)}) %all-gather.10.cloned.1.call-update) | async-done | bytes 3670032 | tf_op jit(solution)/shard_map/all_gather | solution.py:221
  292.8 7.1 %convolution_convert_fusion.4 = bf16[1024,1024]{1,0:T(8,128)(2,1)S(1)} fusion(bf16[1024,1792]{1,0:T(8,128)(2,1)} %all-gather.10.cloned.1.call-done, bf16[1792,1024]{1,0:T(8,128)(2,1)} %param.25), kind=kOutput, calls=%fused_computation.26 | convolution fusion | flops 3759144960 | bytes 9437184 | tf_op jit(solution)/shard_map/dot_general | solution.py:222
  299.9 1.5 copy.64
  301.5 7.2 %all-to-all-start.4 = ((bf16[16,64,1024]{2,1,0:T(8,128)(2,1)}), bf16[16,64,1024]{2,1,0:T(8,128)(2,1)}, u32[]{:S(2)}, u32[]{:S(2)}) async-start(bf16[16,64,1024]{2,1,0:T(8,128)(2,1)} %bitcast.59), calls=%async_computation.6 | async-start | bytes 4194304 | tf_op jit(solution)/shard_map/all_to_all | solution.py:72
  308.6 33.5 %all-to-all-done.4 = bf16[16,64,1024]{2,1,0:T(8,128)(2,1)} async-done(((bf16[16,64,1024]{2,1,0:T(8,128)(2,1)}), bf16[16,64,1024]{2,1,0:T(8,128)(2,1)}, u32[]{:S(2)}, u32[]{:S(2)}) %all-to-all-start.4) | async-done | bytes 2097184 | tf_op jit(solution)/shard_map/all_to_all | solution.py:72
  342.1 2.0 convert_reduce_fusion
  344.1 0.7 add_convert_fusion.1
  (76 shorter events, 4.2 us)
Async XLA Ops:
  6.5 108.8 %copy-start = (bf16[512,1024]{1,0:T(8,128)(2,1)S(1)}, bf16[512,1024]{1,0:T(8,128)(2,1)}, u32[]{:S(2)}) copy-start(bf16[512,1024]{1,0:T(8,128)(2,1)} %param.21) | copy-start | bytes 3145732
  6.5 3.0 copy-start.4
  6.5 6.4 %copy-start.2 = (bf16[2,128,512]{2,1,0:T(8,128)(2,1)S(1)}, bf16[2,128,512]{2,1,0:T(8,128)(2,1)}, u32[]{:S(2)}) copy-start(bf16[2,128,512]{2,1,0:T(8,128)(2,1)} %param.13) | copy-start | bytes 786436
  6.5 32.9 %all-gather.6.cloned.1.call-start = ((), (), s32[]{:S(2)}) async-start(), calls=%async_computation.7 | async-start | bytes 2359296 | tf_op jit(solution)/shard_map/all_gather | solution.py:157
  11.6 57.2 %all-gather.12.cloned.1.call-start = ((), (), s32[]{:S(2)}) async-start(), calls=%async_computation.12 | async-start | bytes 2359296 | tf_op jit(solution)/shard_map/all_gather | solution.py:158
  12.4 2.8 copy-start.3
  12.4 2.8 copy-start.5
  12.4 97.1 %all-gather.8.cloned.1.call-start = ((), (), s32[]{:S(2)}) async-start(), calls=%async_computation.8 | async-start | bytes 2359296 | tf_op jit(solution)/shard_map/all_gather | solution.py:177
  142.1 41.4 %copy-start.9 = (f32[1024]{0:T(1024)S(1)}, f32[1024]{0:T(1024)}, u32[]{:S(2)}) copy-start(f32[1024]{0:T(1024)} %param.22) | copy-start | bytes 12292
  142.1 20.5 %all-to-all-start = ((bf16[16,32,1024]{2,1,0:T(8,128)(2,1)}), bf16[16,32,1024]{2,1,0:T(8,128)(2,1)S(1)}, u32[]{:S(2)}, u32[]{:S(2)}) async-start(bf16[16,32,1024]{2,1,0:T(8,128)(2,1)} %bitcast.16), calls=%async_computation | async-start | bytes 2097152 | tf_op jit(solution)/shard_map/all_to_all | solution.py:72
  145.9 85.1 %reduce-scatter.3.cloned.1.call-start = ((), (), s32[]{:S(2)}) async-start(), calls=%async_computation.9 | async-start | bytes 4128768 | tf_op jit(solution)/shard_map/reduce_scatter | solution.py:199
  162.6 20.9 %copy-start.6 = (bf16[1024,1792]{1,0:T(8,128)(2,1)S(1)}, bf16[1024,1792]{1,0:T(8,128)(2,1)}, u32[]{:S(2)}) copy-start(bf16[1024,1792]{1,0:T(8,128)(2,1)} %param.24) | copy-start | bytes 11010052
  183.6 2.1 copy-start.7
  189.9 71.9 %reduce-scatter.5.cloned.1.call-start = ((), (), s32[]{:S(2)}) async-start(), calls=%async_computation.10 | async-start | bytes 4128768 | tf_op jit(solution)/shard_map/reduce_scatter | solution.py:199
  209.3 4.3 %copy-start.8 = (bf16[1024,1792]{1,0:T(8,128)(2,1)S(1)}, bf16[1024,1792]{1,0:T(8,128)(2,1)}, u32[]{:S(2)}) copy-start(bf16[1024,1792]{1,0:T(8,128)(2,1)} %param.23) | copy-start | bytes 11010052
  217.8 75.0 %all-gather.10.cloned.1.call-start = ((), (), s32[]{:S(2)}) async-start(), calls=%async_computation.11 | async-start | bytes 4128768 | tf_op jit(solution)/shard_map/all_gather | solution.py:221
  301.4 43.4 %copy-start.1 = (bf16[512,1024]{1,0:T(8,128)(2,1)S(1)}, bf16[512,1024]{1,0:T(8,128)(2,1)}, u32[]{:S(2)}) copy-start(bf16[512,1024]{1,0:T(8,128)(2,1)} %param.21) | copy-start | bytes 3145732
  301.5 40.6 %all-to-all-start.4 = ((bf16[16,64,1024]{2,1,0:T(8,128)(2,1)}), bf16[16,64,1024]{2,1,0:T(8,128)(2,1)}, u32[]{:S(2)}, u32[]{:S(2)}) async-start(bf16[16,64,1024]{2,1,0:T(8,128)(2,1)} %bitcast.59), calls=%async_computation.6 | async-start | bytes 4194304 | tf_op jit(solution)/shard_map/all_to_all | solution.py:72
Sparse Core Ops, SparseCore 0:
  11.7 27.6 all-gather.5
  41.1 25.5 all-gather.11
  83.8 25.6 all-gather.7
  190.0 33.6 reduce-scatter.2
  226.0 35.7 reduce-scatter.4
  264.1 28.6 all-gather.9

commit v6 on v3

--- a/solution.py
+++ b/solution.py
@@ -105,9 +105,9 @@
     m_ref[...] = m_new
 
 
-def prefix_attention(query_flat, keys, values, q_tile=512, k_tile=1024):
+def prefix_attention(query_flat, keys_values, q_tile=512, k_tile=1024):
     rows = query_flat.shape[0]
-    length = keys.shape[0]
+    length = keys_values.shape[0]
     return pl.pallas_call(
         prefix_kernel,
         out_shape=(
@@ -119,7 +119,7 @@
         in_specs=[
             pl.BlockSpec((q_tile, HD), lambda i, j: (i, 0)),
             pl.BlockSpec((k_tile, HD), lambda i, j: (j, 0)),
-            pl.BlockSpec((k_tile, HD), lambda i, j: (j, 0)),
+            pl.BlockSpec((k_tile, HD), lambda i, j: (j, 1)),
         ],
         out_specs=(
             pl.BlockSpec((q_tile, 1), lambda i, j: (i, 0)),
@@ -127,7 +127,7 @@
             pl.BlockSpec((q_tile, HD), lambda i, j: (i, 0)),
         ),
         compiler_params=pltpu.CompilerParams(dimension_semantics=("parallel", "arbitrary")),
-    )(query_flat, keys, values)
+    )(query_flat, keys_values, keys_values)
 
 
 def on_device(
@@ -194,15 +194,17 @@
     ).astype(jnp.int32)
     logical_block = jnp.sum(block_match * prefix_block[None, :], axis=1)
     pre_pos = (logical_block * PBLK + row_ids % PBLK).astype(jnp.float32)
-    pre_keys = rotate(
-        lax.dynamic_slice_in_dim(prefix_cache[:, 0], kv_head * HD, HD, 1).astype(jnp.float32),
-        pre_pos,
-    ).astype(jnp.bfloat16)
-    pre_values = lax.dynamic_slice_in_dim(prefix_cache[:, 1], kv_head * HD, HD, 1)
+    key_block = lax.dynamic_slice(prefix_cache, (0, 0, kv_head * HD), (local_prefix, 1, HD))
+    pre_keys = rotate(key_block.reshape(local_prefix, HD).astype(jnp.float32), pre_pos).astype(
+        jnp.bfloat16
+    )
+    value_block = lax.dynamic_slice(prefix_cache, (0, 1, kv_head * HD), (local_prefix, 1, HD))
+    pre_values = value_block.reshape(local_prefix, HD)
     query_flat = query_rot.reshape(all_rows, HD)
-    keys_piece = lax.all_gather(pre_keys, "req", axis=0, tiled=True)
-    values_piece = lax.all_gather(pre_values, "req", axis=0, tiled=True)
-    new_max, new_total, new_acc = prefix_attention(query_flat, keys_piece, values_piece)
+    keys_values = lax.all_gather(
+        jnp.concatenate([pre_keys, pre_values], axis=1), "req", axis=0, tiled=True
+    )
+    new_max, new_total, new_acc = prefix_attention(query_flat, keys_values)
     final_state = (new_max.reshape(all_rows), new_total.reshape(all_rows), new_acc)
     final_state = merge_states(final_state, suffix_state)
     final_max, final_total, final_acc = final_state

time: 367 us -> 337 us (0.918)
  waiting for transfers between devices: 166 us -> 147 us
  local copies, waits for them, and re-layouts: 23.3 us -> 11.6 us
    all_gather x2 -> x1, waiting for transfers between devices: 46.4 us -> 28.2 us  [on_device(): lax.all_gather(jnp.concatenate([pre_keys, pre_values], axis=1), 'req', ax...]
    slice x1 -> x0, local copies, waits for them, and re-layouts: 10.1 us -> none  [on_device(): prefix_cache[:, 1]]
  transfers between devices with their start and end apart: 6 -> 5, of which waited for: 6 -> 5; matrix products, arithmetic and copies ran while one was open for 3% -> 2% of each run, Pallas kernels for 0% -> 0%
where the time goes in v6:
time: 337 us; the launch traced here: 336 us
  waiting for transfers between devices  147 us (44%)
  blocking collectives  79.4 us (24%)
  Pallas kernels  32.5 us (10%)
  other arithmetic  22.9 us (7%)
  matrix products  22.2 us (7%)
  between operations  13.5 us (4%)
  local copies, waits for them, and re-layouts  11.6 us (3%)
  starting transfers between devices  7.1 us (2%)
    all_to_all x1, blocking collectives, exchange_sum(): lax.all_to_all(values.reshape(count, values.shape[0] // count, values.sha...  35.6 us
    all_to_all x1, waiting for transfers between devices, exchange_sum(): lax.all_to_all(values.reshape(count, values.shape[0] // count, values.sha...  33.3 us
    pallas_call x1, Pallas kernels, prefix_attention(): pl.pallas_call(prefix_kernel, out_shape=(jax.ShapeDtypeStruct((rows, 1),...  32.5 us
    all_to_all x1, blocking collectives, exchange_gather(): lax.all_to_all(jnp.broadcast_to(values[None], (count,) + values.shape), a...  31.2 us
    reduce_scatter x1, waiting for transfers between devices, on_device(): lax.psum_scatter(jnp.concatenate([gate_part.astype(jnp.bfloat16), up_part...  30.9 us
    all_gather x1, waiting for transfers between devices, on_device(): hidden_all = lax.all_gather(hidden, 'req', axis=0, tiled=True)  29.5 us
    all_gather x1, waiting for transfers between devices, on_device(): lax.all_gather(jnp.concatenate([pre_keys, pre_values], axis=1), 'req', ax...  28.2 us
    all_gather x1, waiting for transfers between devices, on_device(): lax.all_gather(attn_local, 'req', axis=0, tiled=True)  24.9 us
  transfers between devices with their start and end apart: 5, of which 5 were waited for; matrix products, arithmetic and copies ran while one was open for 2% of the time, Pallas kernels for 0%

profile of v6, /device:TPU:0, one launch (start us, length us, event | category | flops | bytes accessed | tf_op | source)
XLA Modules:
  0.0 336.0 jit_solution(17633840631137093565)
XLA Ops:
  6.6 0.8 select_reduce_fusion
  7.5 2.4 constant_dynamic-slice_fusion.1
  10.0 2.4 fusion.14
  12.4 1.0 pad_maximum_fusion.1
  13.5 0.2 copy.66
  13.7 0.2 copy.85
  13.9 0.2 copy.84
  14.2 0.3 multiply_cosine_fusion.1
  14.5 0.1 subtract_convert_fusion
  14.6 0.2 copy.69
  14.9 0.2 copy.70
  15.1 0.2 select_reduce_fusion.4
  15.4 0.9 dynamic-slice_convert_fusion
  16.5 0.4 fusion.46
  16.9 0.1 copy.74
  17.0 1.1 fusion.22
  18.2 0.3 copy.77
  18.6 0.1 copy.79
  18.7 0.2 reshape.371
  18.9 0.2 reshape.372
  19.1 0.9 pad_maximum_fusion.2.q_ref
  20.0 28.2 %all-gather.4.cloned.1.call-done.k_ref.v_ref = bf16[8192,256]{1,0:T(8,128)(2,1)} async-done(((bf16[1024,256]{1,0:T(8,128)(2,1)}), bf16[8192,256]{1,0:T(8,128)(2,1)}) %all-gather.4.cloned.1.call-update) | async-done | bytes 4194320 | tf_op jit(solution)/shard_map/all_gather | solution.py:204
  48.1 32.5 %shard_map.127 = (f32[1024,1]{1,0:T(8,128)}, f32[1024,1]{1,0:T(8,128)}, f32[1024,128]{1,0:T(8,128)}) custom-call(bf16[1024,128]{1,0:T(8,128)(2,1)} %pad_maximum_fusion.2.q_ref, bf16[8192,256]{1,0:T(8,128)(2,1)} %all-gather.4.cloned.1.call-done.k_ref.v_ref, bf16[8192,256]{1,0:T(8,128)(2,1)} %all-gather.4.cloned.1.call-done.k_ref.v_ref), custom_call_target="tpu_custom_call" | custom-call | tf_op jit(solution)/shard_map/pallas_call | solution.py:111
  80.6 1.7 fusion.30
  82.3 1.5 divide_convert_fusion
  83.8 0.9 reshape.354
  85.2 24.9 %all-gather.6.cloned.1.call-done = bf16[2048,512]{1,0:T(8,128)(2,1)} async-done(((bf16[256,512]{1,0:T(8,128)(2,1)}), bf16[2048,512]{1,0:T(8,128)(2,1)}) %all-gather.6.cloned.1.call-update) | async-done | bytes 2097168 | tf_op jit(solution)/shard_map/all_gather | solution.py:219
  110.1 5.8 %gather_fusion = bf16[1024,512]{1,0:T(8,128)(2,1)S(1)} fusion(bf16[2048,512]{1,0:T(8,128)(2,1)} %all-gather.6.cloned.1.call-done, s32[1024]{0:T(1024)S(1)} %broadcast_clamp_fusion), kind=kCustom, calls=%fused_computation | custom fusion | bytes 2101248 | tf_op jit(solution)/shard_map/jit(_take)/gather | solution.py:219
  116.0 2.7 convolution_convert_fusion.3
  118.6 7.0 %all-to-all-start = ((bf16[16,64,1024]{2,1,0:T(8,128)(2,1)}), bf16[16,64,1024]{2,1,0:T(8,128)(2,1)S(1)}, u32[]{:S(2)}, u32[]{:S(2)}) async-start(bf16[16,64,1024]{2,1,0:T(8,128)(2,1)} %bitcast.40), calls=%async_computation | async-start | bytes 4194304 | tf_op jit(solution)/shard_map/all_to_all | solution.py:74
  125.7 33.3 %all-to-all-done = bf16[16,64,1024]{2,1,0:T(8,128)(2,1)S(1)} async-done(((bf16[16,64,1024]{2,1,0:T(8,128)(2,1)}), bf16[16,64,1024]{2,1,0:T(8,128)(2,1)S(1)}, u32[]{:S(2)}, u32[]{:S(2)}) %all-to-all-start) | async-done | bytes 2097184 | tf_op jit(solution)/shard_map/all_to_all | solution.py:74
  159.0 0.4 convert_reduce_fusion.1
  159.4 1.1 add_convert_fusion.2
  160.5 0.3 broadcast_in_dim.25
  160.8 31.2 %all_to_all.15 = bf16[16,64,1024]{2,1,0:T(8,128)(2,1)S(1)} all-to-all(bf16[16,64,1024]{2,1,0:T(8,128)(2,1)S(1)} %broadcast_in_dim.25), channel_id=1, replica_groups=mesh['req'=8,'hid'=16] {'hid'}, dimensions={0} | all-to-all | bytes 4194304 | tf_op jit(solution)/shard_map/all_to_all | solution.py:81
  192.0 5.4 %convolution_convert_fusion = bf16[1024,1792]{1,0:T(8,128)(2,1)} fusion(bf16[1024,1792]{1,0:T(8,128)(2,1)S(1)} %copy-done.5, bf16[1024,1024]{1,0:T(8,128)(2,1)S(1)} %bitcast.36, f32[1024]{0:T(1024)S(1)} %copy-done.7), kind=kOutput, calls=%fused_computation.8 | convolution fusion | flops 3763077120 | bytes 9441280 | tf_op jit(solution)/shard_map/dot_general | solution.py:229
  197.4 5.4 %convolution_convert_fusion.1 = bf16[1024,1792]{1,0:T(8,128)(2,1)} fusion(bf16[1024,1792]{1,0:T(8,128)(2,1)S(1)} %copy-done.6, bf16[1024,1024]{1,0:T(8,128)(2,1)S(1)} %bitcast.37, f32[1024]{0:T(1024)S(1)} %copy-done.7), kind=kOutput, calls=%fused_computation.9 | convolution fusion | flops 3763077120 | bytes 9441280 | tf_op jit(solution)/shard_map/dot_general | solution.py:228
  202.8 6.6 %pad_maximum_fusion = bf16[1024,3584]{1,0:T(8,128)(2,1)} fusion(bf16[1024,1792]{1,0:T(8,128)(2,1)} %convolution_convert_fusion, bf16[1024,1792]{1,0:T(8,128)(2,1)} %convolution_convert_fusion.1), kind=kLoop, calls=%fused_computation.1 | loop fusion | flops 14680064 | bytes 14680064 | tf_op jit(solution)/shard_map/concatenate | solution.py:233
  209.6 0.5 fusion.1
  210.0 12.6 %psum.7 = f32[1024]{0:T(1024)S(1)} all-reduce(f32[1024]{0:T(1024)S(1)} %fusion.1), channel_id=1, replica_groups=mesh['req'=8,'hid'=16] {'req'}, use_global_device_ids=true, to_apply=%region_12.13 | all-reduce | flops 1024 | bytes 8192 | tf_op jit(solution)/shard_map/psum | solution.py:230
  222.8 30.9 %reduce-scatter.2.cloned.1.call-done = bf16[128,3584]{1,0:T(8,128)(2,1)} async-done(((bf16[1024,3584]{1,0:T(8,128)(2,1)}), bf16[128,3584]{1,0:T(8,128)(2,1)}) %reduce-scatter.2.cloned.1.call-update) | async-done | bytes 917520 | tf_op jit(solution)/shard_map/reduce_scatter | solution.py:232
  253.6 1.4 convert_element_type.118
  255.0 1.1 fusion.8
  256.1 29.5 %all-gather.8.cloned.1.call-done = bf16[1024,1792]{1,0:T(8,128)(2,1)} async-done(((bf16[128,1792]{1,0:T(8,128)(2,1)}), bf16[1024,1792]{1,0:T(8,128)(2,1)}) %all-gather.8.cloned.1.call-update) | async-done | bytes 3670032 | tf_op jit(solution)/shard_map/all_gather | solution.py:245
  285.6 7.2 %convolution_convert_fusion.2 = bf16[1024,1024]{1,0:T(8,128)(2,1)S(1)} fusion(bf16[1024,1792]{1,0:T(8,128)(2,1)} %all-gather.8.cloned.1.call-done, bf16[1792,1024]{1,0:T(8,128)(2,1)} %param.25), kind=kOutput, calls=%fused_computation.10 | convolution fusion | flops 3759144960 | bytes 9437184 | tf_op jit(solution)/shard_map/dot_general | solution.py:247
  292.8 35.6 %all_to_all.16 = bf16[16,64,1024]{2,1,0:T(8,128)(2,1)S(1)} all-to-all(bf16[16,64,1024]{2,1,0:T(8,128)(2,1)S(1)} %bitcast.41), channel_id=1, replica_groups=mesh['req'=8,'hid'=16] {'hid'}, dimensions={0} | all-to-all | bytes 4194304 | tf_op jit(solution)/shard_map/all_to_all | solution.py:74
  328.4 0.4 convert_reduce_fusion
  328.8 0.7 add_convert_fusion.1
  (48 shorter events, 1.4 us)
Async XLA Ops:
  6.5 109.4 %copy-start = (bf16[512,1024]{1,0:T(8,128)(2,1)S(1)}, bf16[512,1024]{1,0:T(8,128)(2,1)}, u32[]{:S(2)}) copy-start(bf16[512,1024]{1,0:T(8,128)(2,1)} %param.21) | copy-start | bytes 3145732
  6.5 41.6 %all-gather.4.cloned.1.call-start = ((), (), s32[]{:S(2)}) async-start(), calls=%async_computation.4 | async-start | bytes 4718592 | tf_op jit(solution)/shard_map/all_gather | solution.py:204
  7.4 6.1 %copy-start.2 = (bf16[2,128,512]{2,1,0:T(8,128)(2,1)S(1)}, bf16[2,128,512]{2,1,0:T(8,128)(2,1)}, u32[]{:S(2)}) copy-start(bf16[2,128,512]{2,1,0:T(8,128)(2,1)} %param.13) | copy-start | bytes 786436
  12.4 2.7 copy-start.3
  12.4 2.7 copy-start.4
  13.5 96.7 %all-gather.6.cloned.1.call-start = ((), (), s32[]{:S(2)}) async-start(), calls=%async_computation.5 | async-start | bytes 2359296 | tf_op jit(solution)/shard_map/all_gather | solution.py:219
  118.6 40.4 %all-to-all-start = ((bf16[16,64,1024]{2,1,0:T(8,128)(2,1)}), bf16[16,64,1024]{2,1,0:T(8,128)(2,1)S(1)}, u32[]{:S(2)}, u32[]{:S(2)}) async-start(bf16[16,64,1024]{2,1,0:T(8,128)(2,1)} %bitcast.40), calls=%async_computation | async-start | bytes 4194304 | tf_op jit(solution)/shard_map/all_to_all | solution.py:74
  125.6 128.0 %reduce-scatter.2.cloned.1.call-start = ((), (), s32[]{:S(2)}) async-start(), calls=%async_computation.6 | async-start | bytes 8257536 | tf_op jit(solution)/shard_map/reduce_scatter | solution.py:232
  159.4 32.5 %copy-start.5 = (bf16[1024,1792]{1,0:T(8,128)(2,1)S(1)}, bf16[1024,1792]{1,0:T(8,128)(2,1)}, u32[]{:S(2)}) copy-start(bf16[1024,1792]{1,0:T(8,128)(2,1)} %param.24) | copy-start | bytes 11010052
  159.4 32.5 %copy-start.7 = (f32[1024]{0:T(1024)S(1)}, f32[1024]{0:T(1024)}, u32[]{:S(2)}) copy-start(f32[1024]{0:T(1024)} %param.22) | copy-start | bytes 12292
  191.9 5.4 %copy-start.6 = (bf16[1024,1792]{1,0:T(8,128)(2,1)S(1)}, bf16[1024,1792]{1,0:T(8,128)(2,1)}, u32[]{:S(2)}) copy-start(bf16[1024,1792]{1,0:T(8,128)(2,1)} %param.23) | copy-start | bytes 11010052
  209.5 76.1 %all-gather.8.cloned.1.call-start = ((), (), s32[]{:S(2)}) async-start(), calls=%async_computation.7 | async-start | bytes 4128768 | tf_op jit(solution)/shard_map/all_gather | solution.py:245
  285.6 43.8 %copy-start.1 = (bf16[512,1024]{1,0:T(8,128)(2,1)S(1)}, bf16[512,1024]{1,0:T(8,128)(2,1)}, u32[]{:S(2)}) copy-start(bf16[512,1024]{1,0:T(8,128)(2,1)} %param.21) | copy-start | bytes 3145732
Sparse Core Ops, SparseCore 0:
  13.6 34.5 all-gather.3
  84.8 25.2 all-gather.5
  209.6 43.9 reduce-scatter.1
  256.2 29.3 all-gather.7

commit v7 on v6

--- a/solution.py
+++ b/solution.py
@@ -105,7 +105,7 @@
     m_ref[...] = m_new
 
 
-def prefix_attention(query_flat, keys_values, q_tile=512, k_tile=1024):
+def prefix_attention(query_flat, keys_values, q_tile=512, k_tile=4096):
     rows = query_flat.shape[0]
     length = keys_values.shape[0]
     return pl.pallas_call(

time: 337 us -> 323 us (0.958)
  Pallas kernels: 32.5 us -> 18.5 us
    pallas_call x1, Pallas kernels: 32.5 us -> 18.5 us  [prefix_attention(): pl.pallas_call(prefix_kernel, out_shape=(jax.ShapeDtypeStruct((rows, 1),...]
where the time goes in v7:
time: 323 us; the launch traced here: 322 us
  waiting for transfers between devices  147 us (46%)
  blocking collectives  79.4 us (25%)
  other arithmetic  22.9 us (7%)
  matrix products  22.2 us (7%)
  Pallas kernels  18.5 us (6%)
  between operations  13.5 us (4%)
  local copies, waits for them, and re-layouts  11.6 us (4%)
  starting transfers between devices  7.29 us (2%)
    all_to_all x1, blocking collectives, exchange_sum(): lax.all_to_all(values.reshape(count, values.shape[0] // count, values.sha...  35.6 us
    all_to_all x1, waiting for transfers between devices, exchange_sum(): lax.all_to_all(values.reshape(count, values.shape[0] // count, values.sha...  33.4 us
    all_to_all x1, blocking collectives, exchange_gather(): lax.all_to_all(jnp.broadcast_to(values[None], (count,) + values.shape), a...  31.2 us
    reduce_scatter x1, waiting for transfers between devices, on_device(): lax.psum_scatter(jnp.concatenate([gate_part.astype(jnp.bfloat16), up_part...  30.8 us
    all_gather x1, waiting for transfers between devices, on_device(): hidden_all = lax.all_gather(hidden, 'req', axis=0, tiled=True)  29.6 us
    all_gather x1, waiting for transfers between devices, on_device(): lax.all_gather(jnp.concatenate([pre_keys, pre_values], axis=1), 'req', ax...  28 us
    all_gather x1, waiting for transfers between devices, on_device(): lax.all_gather(attn_local, 'req', axis=0, tiled=True)  24.9 us
    pallas_call x1, Pallas kernels, prefix_attention(): pl.pallas_call(prefix_kernel, out_shape=(jax.ShapeDtypeStruct((rows, 1),...  18.5 us
  transfers between devices with their start and end apart: 5, of which 5 were waited for; matrix products, arithmetic and copies ran while one was open for 2% of the time, Pallas kernels for 0%

profile of v7, /device:TPU:0, one launch (start us, length us, event | category | flops | bytes accessed | tf_op | source)
XLA Modules:
  0.0 322.2 jit_solution(11255760138750903939)
XLA Ops:
  6.6 0.8 select_reduce_fusion
  7.5 2.4 constant_dynamic-slice_fusion.1
  10.0 2.4 fusion.14
  12.4 1.0 pad_maximum_fusion.1
  13.5 0.2 all-gather.6.cloned.1.call-start
  13.7 0.2 copy.66
  13.9 0.2 copy.85
  14.1 0.2 copy.84
  14.3 0.3 multiply_cosine_fusion.1
  14.7 0.1 subtract_convert_fusion
  14.8 0.2 copy.69
  15.0 0.2 copy.70
  15.3 0.2 select_reduce_fusion.4
  15.5 0.9 dynamic-slice_convert_fusion
  16.7 0.4 fusion.46
  17.1 0.1 copy.74
  17.2 1.1 fusion.22
  18.3 0.3 copy.77
  18.9 0.2 reshape.371
  19.1 0.2 reshape.372
  19.3 0.9 pad_maximum_fusion.2.q_ref
  20.1 28.0 %all-gather.4.cloned.1.call-done.k_ref.v_ref = bf16[8192,256]{1,0:T(8,128)(2,1)} async-done(((bf16[1024,256]{1,0:T(8,128)(2,1)}), bf16[8192,256]{1,0:T(8,128)(2,1)}) %all-gather.4.cloned.1.call-update) | async-done | bytes 4194320 | tf_op jit(solution)/shard_map/all_gather | solution.py:204
  48.1 18.5 %shard_map.127 = (f32[1024,1]{1,0:T(8,128)}, f32[1024,1]{1,0:T(8,128)}, f32[1024,128]{1,0:T(8,128)}) custom-call(bf16[1024,128]{1,0:T(8,128)(2,1)} %pad_maximum_fusion.2.q_ref, bf16[8192,256]{1,0:T(8,128)(2,1)} %all-gather.4.cloned.1.call-done.k_ref.v_ref, bf16[8192,256]{1,0:T(8,128)(2,1)} %all-gather.4.cloned.1.call-done.k_ref.v_ref), custom_call_target="tpu_custom_call" | custom-call | tf_op jit(solution)/shard_map/pallas_call | solution.py:111
  66.7 1.7 fusion.30
  68.4 1.5 divide_convert_fusion
  69.9 0.9 reshape.354
  71.3 24.9 %all-gather.6.cloned.1.call-done = bf16[2048,512]{1,0:T(8,128)(2,1)} async-done(((bf16[256,512]{1,0:T(8,128)(2,1)}), bf16[2048,512]{1,0:T(8,128)(2,1)}) %all-gather.6.cloned.1.call-update) | async-done | bytes 2097168 | tf_op jit(solution)/shard_map/all_gather | solution.py:219
  96.2 5.8 %gather_fusion = bf16[1024,512]{1,0:T(8,128)(2,1)S(1)} fusion(bf16[2048,512]{1,0:T(8,128)(2,1)} %all-gather.6.cloned.1.call-done, s32[1024]{0:T(1024)S(1)} %broadcast_clamp_fusion), kind=kCustom, calls=%fused_computation | custom fusion | bytes 2101248 | tf_op jit(solution)/shard_map/jit(_take)/gather | solution.py:219
  102.1 2.7 convolution_convert_fusion.3
  104.7 7.0 %all-to-all-start = ((bf16[16,64,1024]{2,1,0:T(8,128)(2,1)}), bf16[16,64,1024]{2,1,0:T(8,128)(2,1)S(1)}, u32[]{:S(2)}, u32[]{:S(2)}) async-start(bf16[16,64,1024]{2,1,0:T(8,128)(2,1)} %bitcast.40), calls=%async_computation | async-start | bytes 4194304 | tf_op jit(solution)/shard_map/all_to_all | solution.py:74
  111.8 33.4 %all-to-all-done = bf16[16,64,1024]{2,1,0:T(8,128)(2,1)S(1)} async-done(((bf16[16,64,1024]{2,1,0:T(8,128)(2,1)}), bf16[16,64,1024]{2,1,0:T(8,128)(2,1)S(1)}, u32[]{:S(2)}, u32[]{:S(2)}) %all-to-all-start) | async-done | bytes 2097184 | tf_op jit(solution)/shard_map/all_to_all | solution.py:74
  145.1 0.4 convert_reduce_fusion.1
  145.5 1.1 add_convert_fusion.2
  146.6 0.3 broadcast_in_dim.25
  146.9 31.2 %all_to_all.15 = bf16[16,64,1024]{2,1,0:T(8,128)(2,1)S(1)} all-to-all(bf16[16,64,1024]{2,1,0:T(8,128)(2,1)S(1)} %broadcast_in_dim.25), channel_id=1, replica_groups=mesh['req'=8,'hid'=16] {'hid'}, dimensions={0} | all-to-all | bytes 4194304 | tf_op jit(solution)/shard_map/all_to_all | solution.py:81
  178.1 5.4 %convolution_convert_fusion = bf16[1024,1792]{1,0:T(8,128)(2,1)} fusion(bf16[1024,1792]{1,0:T(8,128)(2,1)S(1)} %copy-done.5, bf16[1024,1024]{1,0:T(8,128)(2,1)S(1)} %bitcast.36, f32[1024]{0:T(1024)S(1)} %copy-done.7), kind=kOutput, calls=%fused_computation.8 | convolution fusion | flops 3763077120 | bytes 9441280 | tf_op jit(solution)/shard_map/dot_general | solution.py:229
  183.5 5.4 %convolution_convert_fusion.1 = bf16[1024,1792]{1,0:T(8,128)(2,1)} fusion(bf16[1024,1792]{1,0:T(8,128)(2,1)S(1)} %copy-done.6, bf16[1024,1024]{1,0:T(8,128)(2,1)S(1)} %bitcast.37, f32[1024]{0:T(1024)S(1)} %copy-done.7), kind=kOutput, calls=%fused_computation.9 | convolution fusion | flops 3763077120 | bytes 9441280 | tf_op jit(solution)/shard_map/dot_general | solution.py:228
  189.0 6.6 %pad_maximum_fusion = bf16[1024,3584]{1,0:T(8,128)(2,1)} fusion(bf16[1024,1792]{1,0:T(8,128)(2,1)} %convolution_convert_fusion, bf16[1024,1792]{1,0:T(8,128)(2,1)} %convolution_convert_fusion.1), kind=kLoop, calls=%fused_computation.1 | loop fusion | flops 14680064 | bytes 14680064 | tf_op jit(solution)/shard_map/concatenate | solution.py:233
  195.7 0.5 fusion.1
  196.2 12.6 %psum.7 = f32[1024]{0:T(1024)S(1)} all-reduce(f32[1024]{0:T(1024)S(1)} %fusion.1), channel_id=1, replica_groups=mesh['req'=8,'hid'=16] {'req'}, use_global_device_ids=true, to_apply=%region_12.13 | all-reduce | flops 1024 | bytes 8192 | tf_op jit(solution)/shard_map/psum | solution.py:230
  208.9 30.8 %reduce-scatter.2.cloned.1.call-done = bf16[128,3584]{1,0:T(8,128)(2,1)} async-done(((bf16[1024,3584]{1,0:T(8,128)(2,1)}), bf16[128,3584]{1,0:T(8,128)(2,1)}) %reduce-scatter.2.cloned.1.call-update) | async-done | bytes 917520 | tf_op jit(solution)/shard_map/reduce_scatter | solution.py:232
  239.7 1.4 convert_element_type.118
  241.1 1.1 fusion.8
  242.2 29.6 %all-gather.8.cloned.1.call-done = bf16[1024,1792]{1,0:T(8,128)(2,1)} async-done(((bf16[128,1792]{1,0:T(8,128)(2,1)}), bf16[1024,1792]{1,0:T(8,128)(2,1)}) %all-gather.8.cloned.1.call-update) | async-done | bytes 3670032 | tf_op jit(solution)/shard_map/all_gather | solution.py:245
  271.8 7.2 %convolution_convert_fusion.2 = bf16[1024,1024]{1,0:T(8,128)(2,1)S(1)} fusion(bf16[1024,1792]{1,0:T(8,128)(2,1)} %all-gather.8.cloned.1.call-done, bf16[1792,1024]{1,0:T(8,128)(2,1)} %param.25), kind=kOutput, calls=%fused_computation.10 | convolution fusion | flops 3759144960 | bytes 9437184 | tf_op jit(solution)/shard_map/dot_general | solution.py:247
  279.0 35.6 %all_to_all.16 = bf16[16,64,1024]{2,1,0:T(8,128)(2,1)S(1)} all-to-all(bf16[16,64,1024]{2,1,0:T(8,128)(2,1)S(1)} %bitcast.41), channel_id=1, replica_groups=mesh['req'=8,'hid'=16] {'hid'}, dimensions={0} | all-to-all | bytes 4194304 | tf_op jit(solution)/shard_map/all_to_all | solution.py:74
  314.5 0.4 convert_reduce_fusion
  314.9 0.7 add_convert_fusion.1
  (48 shorter events, 1.5 us)
Async XLA Ops:
  6.5 95.5 %copy-start = (bf16[512,1024]{1,0:T(8,128)(2,1)S(1)}, bf16[512,1024]{1,0:T(8,128)(2,1)}, u32[]{:S(2)}) copy-start(bf16[512,1024]{1,0:T(8,128)(2,1)} %param.21) | copy-start | bytes 3145732
  6.5 41.6 %all-gather.4.cloned.1.call-start = ((), (), s32[]{:S(2)}) async-start(), calls=%async_computation.4 | async-start | bytes 4718592 | tf_op jit(solution)/shard_map/all_gather | solution.py:204
  7.4 6.2 %copy-start.2 = (bf16[2,128,512]{2,1,0:T(8,128)(2,1)S(1)}, bf16[2,128,512]{2,1,0:T(8,128)(2,1)}, u32[]{:S(2)}) copy-start(bf16[2,128,512]{2,1,0:T(8,128)(2,1)} %param.13) | copy-start | bytes 786436
  12.4 2.9 copy-start.3
  12.4 2.9 copy-start.4
  13.5 82.7 %all-gather.6.cloned.1.call-start = ((), (), s32[]{:S(2)}) async-start(), calls=%async_computation.5 | async-start | bytes 2359296 | tf_op jit(solution)/shard_map/all_gather | solution.py:219
  104.7 40.4 %all-to-all-start = ((bf16[16,64,1024]{2,1,0:T(8,128)(2,1)}), bf16[16,64,1024]{2,1,0:T(8,128)(2,1)S(1)}, u32[]{:S(2)}, u32[]{:S(2)}) async-start(bf16[16,64,1024]{2,1,0:T(8,128)(2,1)} %bitcast.40), calls=%async_computation | async-start | bytes 4194304 | tf_op jit(solution)/shard_map/all_to_all | solution.py:74
  111.7 128.0 %reduce-scatter.2.cloned.1.call-start = ((), (), s32[]{:S(2)}) async-start(), calls=%async_computation.6 | async-start | bytes 8257536 | tf_op jit(solution)/shard_map/reduce_scatter | solution.py:232
  145.5 32.6 %copy-start.5 = (bf16[1024,1792]{1,0:T(8,128)(2,1)S(1)}, bf16[1024,1792]{1,0:T(8,128)(2,1)}, u32[]{:S(2)}) copy-start(bf16[1024,1792]{1,0:T(8,128)(2,1)} %param.24) | copy-start | bytes 11010052
  145.5 32.6 %copy-start.7 = (f32[1024]{0:T(1024)S(1)}, f32[1024]{0:T(1024)}, u32[]{:S(2)}) copy-start(f32[1024]{0:T(1024)} %param.22) | copy-start | bytes 12292
  178.1 5.4 %copy-start.6 = (bf16[1024,1792]{1,0:T(8,128)(2,1)S(1)}, bf16[1024,1792]{1,0:T(8,128)(2,1)}, u32[]{:S(2)}) copy-start(bf16[1024,1792]{1,0:T(8,128)(2,1)} %param.23) | copy-start | bytes 11010052
  195.6 76.1 %all-gather.8.cloned.1.call-start = ((), (), s32[]{:S(2)}) async-start(), calls=%async_computation.7 | async-start | bytes 4128768 | tf_op jit(solution)/shard_map/all_gather | solution.py:245
  271.8 43.8 %copy-start.1 = (bf16[512,1024]{1,0:T(8,128)(2,1)S(1)}, bf16[512,1024]{1,0:T(8,128)(2,1)}, u32[]{:S(2)}) copy-start(bf16[512,1024]{1,0:T(8,128)(2,1)} %param.21) | copy-start | bytes 3145732
Sparse Core Ops, SparseCore 0:
  13.6 34.5 all-gather.3
  70.9 25.2 all-gather.5
  195.8 43.9 reduce-scatter.1
  242.3 29.3 all-gather.7

commit v8 on v7

--- a/solution.py
+++ b/solution.py
@@ -216,7 +216,11 @@
     tokens = residual.shape[0]
     own_rows = tokens // hid_count
     source = token_source(suffix_len, slot_request, tokens, maxlen)
-    token_rows = jnp.take(lax.all_gather(attn_local, "req", axis=0, tiled=True), source, axis=0)
+    attn_all = lax.all_gather(attn_local, "req", axis=0, tiled=True)
+    pick = (source[:, None] == jnp.arange(attn_all.shape[0], dtype=jnp.int32)[None, :]).astype(
+        jnp.bfloat16
+    )
+    token_rows = jnp.dot(pick, attn_all, preferred_element_type=jnp.float32).astype(jnp.bfloat16)
     projected = jnp.dot(token_rows, out_weight, preferred_element_type=jnp.float32)
     summed = exchange_sum(projected.astype(jnp.bfloat16), "hid", hid_count)
     residual_own = lax.dynamic_slice_in_dim(residual, hid_index * own_rows, own_rows, 0)

time: 323 us -> 320 us (level)
  local copies, waits for them, and re-layouts: 11.6 us -> 5.79 us
  matrix products: 22.2 us -> 25.9 us
    gather x1 -> x0, local copies, waits for them, and re-layouts: 5.85 us -> none  [on_device(): jnp.take(lax.all_gather(attn_local, 'req', axis=0, tiled=True), source, a...]
    dot_general x1, matrix products: 2.66 us -> 6.35 us  [on_device(): jnp.dot(token_rows, out_weight, preferred_element_type=jnp.float32)]
where the time goes in v8:
time: 320 us
  waiting for transfers between devices  146 us (46%)
  blocking collectives  79.4 us (25%)
  matrix products  25.9 us (8%)
  other arithmetic  22.9 us (7%)
  Pallas kernels  18.5 us (6%)
  between operations  13.4 us (4%)
  starting transfers between devices  7.51 us (2%)
  local copies, waits for them, and re-layouts  5.79 us (2%)
    all_to_all x1, blocking collectives, exchange_sum(): lax.all_to_all(values.reshape(count, values.shape[0] // count, values.sha...  35.6 us
    all_to_all x1, waiting for transfers between devices, exchange_sum(): lax.all_to_all(values.reshape(count, values.shape[0] // count, values.sha...  33.1 us
    all_to_all x1, blocking collectives, exchange_gather(): lax.all_to_all(jnp.broadcast_to(values[None], (count,) + values.shape), a...  31.2 us
    reduce_scatter x1, waiting for transfers between devices, on_device(): lax.psum_scatter(jnp.concatenate([gate_part.astype(jnp.bfloat16), up_part...  30.8 us
    all_gather x1, waiting for transfers between devices, on_device(): hidden_all = lax.all_gather(hidden, 'req', axis=0, tiled=True)  29.5 us
    all_gather x1, waiting for transfers between devices, on_device(): lax.all_gather(jnp.concatenate([pre_keys, pre_values], axis=1), 'req', ax...  28 us
    all_gather x1, waiting for transfers between devices, on_device(): attn_all = lax.all_gather(attn_local, 'req', axis=0, tiled=True)  24.9 us
    pallas_call x1, Pallas kernels, prefix_attention(): pl.pallas_call(prefix_kernel, out_shape=(jax.ShapeDtypeStruct((rows, 1),...  18.5 us
  transfers between devices with their start and end apart: 5, of which 5 were waited for; matrix products, arithmetic and copies ran while one was open for 2% of the time, Pallas kernels for 0%

profile of v8, /device:TPU:0, one launch (start us, length us, event | category | flops | bytes accessed | tf_op | source)
XLA Modules:
  0.0 319.9 jit_solution(6679795036373244722)
XLA Ops:
  6.6 0.8 select_reduce_fusion
  7.5 2.4 constant_dynamic-slice_fusion.1
  10.0 2.4 fusion.15
  12.4 1.0 pad_maximum_fusion.1
  13.5 0.2 all-gather.6.cloned.1.call-start
  13.7 0.2 copy.66
  13.9 0.2 copy.85
  14.1 0.2 copy.84
  14.3 0.3 multiply_cosine_fusion.1
  14.7 0.1 subtract_convert_fusion
  14.8 0.2 copy.69
  15.0 0.2 copy.70
  15.3 0.2 select_reduce_fusion.4
  15.5 0.9 dynamic-slice_convert_fusion
  16.7 0.4 fusion.45
  17.1 0.1 copy.74
  17.2 1.1 fusion.22
  18.3 0.3 copy.77
  18.9 0.2 reshape.334
  19.1 0.2 reshape.335
  19.3 0.9 pad_maximum_fusion.2.q_ref
  20.1 28.0 %all-gather.4.cloned.1.call-done.k_ref.v_ref = bf16[8192,256]{1,0:T(8,128)(2,1)} async-done(((bf16[1024,256]{1,0:T(8,128)(2,1)}), bf16[8192,256]{1,0:T(8,128)(2,1)}) %all-gather.4.cloned.1.call-update) | async-done | bytes 4194320 | tf_op jit(solution)/shard_map/all_gather | solution.py:204
  48.1 18.5 %shard_map.127 = (f32[1024,1]{1,0:T(8,128)}, f32[1024,1]{1,0:T(8,128)}, f32[1024,128]{1,0:T(8,128)}) custom-call(bf16[1024,128]{1,0:T(8,128)(2,1)} %pad_maximum_fusion.2.q_ref, bf16[8192,256]{1,0:T(8,128)(2,1)} %all-gather.4.cloned.1.call-done.k_ref.v_ref, bf16[8192,256]{1,0:T(8,128)(2,1)} %all-gather.4.cloned.1.call-done.k_ref.v_ref), custom_call_target="tpu_custom_call" | custom-call | tf_op jit(solution)/shard_map/pallas_call | solution.py:111
  66.7 1.7 fusion.30
  68.4 1.5 divide_convert_fusion
  69.9 0.9 reshape.325
  71.3 24.9 %all-gather.6.cloned.1.call-done = bf16[2048,512]{1,0:T(8,128)(2,1)} async-done(((bf16[256,512]{1,0:T(8,128)(2,1)}), bf16[2048,512]{1,0:T(8,128)(2,1)}) %all-gather.6.cloned.1.call-update) | async-done | bytes 2097168 | tf_op jit(solution)/shard_map/all_gather | solution.py:219
  96.2 6.3 %convolution_convert_fusion.3 = bf16[1024,1024]{1,0:T(8,128)(2,1)} fusion(bf16[512,1024]{1,0:T(8,128)(2,1)S(1)} %copy-done, bf16[2048,512]{1,0:T(8,128)(2,1)} %all-gather.6.cloned.1.call-done, s32[1024]{0:T(1024)S(1)} %add_subtract_fusion), kind=kOutput, calls=%fused_computation.13 | convolution fusion | flops 3224895488 | bytes 5246976 | tf_op jit(solution)/shard_map/dot_general | solution.py:224
  102.5 7.0 %all-to-all-start = ((bf16[16,64,1024]{2,1,0:T(8,128)(2,1)}), bf16[16,64,1024]{2,1,0:T(8,128)(2,1)S(1)}, u32[]{:S(2)}, u32[]{:S(2)}) async-start(bf16[16,64,1024]{2,1,0:T(8,128)(2,1)} %bitcast.38), calls=%async_computation | async-start | bytes 4194304 | tf_op jit(solution)/shard_map/all_to_all | solution.py:74
  109.5 0.3 reduce-scatter.2.cloned.1.call-start
  109.8 33.1 %all-to-all-done = bf16[16,64,1024]{2,1,0:T(8,128)(2,1)S(1)} async-done(((bf16[16,64,1024]{2,1,0:T(8,128)(2,1)}), bf16[16,64,1024]{2,1,0:T(8,128)(2,1)S(1)}, u32[]{:S(2)}, u32[]{:S(2)}) %all-to-all-start) | async-done | bytes 2097184 | tf_op jit(solution)/shard_map/all_to_all | solution.py:74
  142.9 0.4 convert_reduce_fusion.1
  143.3 1.1 add_convert_fusion.2
  144.4 0.3 broadcast_in_dim.12
  144.7 31.2 %all_to_all.15 = bf16[16,64,1024]{2,1,0:T(8,128)(2,1)S(1)} all-to-all(bf16[16,64,1024]{2,1,0:T(8,128)(2,1)S(1)} %broadcast_in_dim.12), channel_id=1, replica_groups=mesh['req'=8,'hid'=16] {'hid'}, dimensions={0} | all-to-all | bytes 4194304 | tf_op jit(solution)/shard_map/all_to_all | solution.py:81
  175.9 5.4 %convolution_convert_fusion = bf16[1024,1792]{1,0:T(8,128)(2,1)} fusion(bf16[1024,1792]{1,0:T(8,128)(2,1)S(1)} %copy-done.5, bf16[1024,1024]{1,0:T(8,128)(2,1)S(1)} %bitcast.34, f32[1024]{0:T(1024)S(1)} %copy-done.7), kind=kOutput, calls=%fused_computation.10 | convolution fusion | flops 3763077120 | bytes 9441280 | tf_op jit(solution)/shard_map/dot_general | solution.py:233
  181.3 5.4 %convolution_convert_fusion.1 = bf16[1024,1792]{1,0:T(8,128)(2,1)} fusion(bf16[1024,1792]{1,0:T(8,128)(2,1)S(1)} %copy-done.6, bf16[1024,1024]{1,0:T(8,128)(2,1)S(1)} %bitcast.35, f32[1024]{0:T(1024)S(1)} %copy-done.7), kind=kOutput, calls=%fused_computation.11 | convolution fusion | flops 3763077120 | bytes 9441280 | tf_op jit(solution)/shard_map/dot_general | solution.py:232
  186.8 6.6 %pad_maximum_fusion = bf16[1024,3584]{1,0:T(8,128)(2,1)} fusion(bf16[1024,1792]{1,0:T(8,128)(2,1)} %convolution_convert_fusion, bf16[1024,1792]{1,0:T(8,128)(2,1)} %convolution_convert_fusion.1), kind=kLoop, calls=%fused_computation.2 | loop fusion | flops 14680064 | bytes 14680064 | tf_op jit(solution)/shard_map/concatenate | solution.py:237
  193.5 0.5 fusion.2
  194.0 12.6 %psum.7 = f32[1024]{0:T(1024)S(1)} all-reduce(f32[1024]{0:T(1024)S(1)} %fusion.2), channel_id=1, replica_groups=mesh['req'=8,'hid'=16] {'req'}, use_global_device_ids=true, to_apply=%region_12.13 | all-reduce | flops 1024 | bytes 8192 | tf_op jit(solution)/shard_map/psum | solution.py:234
  206.7 30.8 %reduce-scatter.2.cloned.1.call-done = bf16[128,3584]{1,0:T(8,128)(2,1)} async-done(((bf16[1024,3584]{1,0:T(8,128)(2,1)}), bf16[128,3584]{1,0:T(8,128)(2,1)}) %reduce-scatter.2.cloned.1.call-update) | async-done | bytes 917520 | tf_op jit(solution)/shard_map/reduce_scatter | solution.py:236
  237.5 1.4 convert_element_type.123
  238.9 1.1 fusion.9
  240.0 29.5 %all-gather.8.cloned.1.call-done = bf16[1024,1792]{1,0:T(8,128)(2,1)} async-done(((bf16[128,1792]{1,0:T(8,128)(2,1)}), bf16[1024,1792]{1,0:T(8,128)(2,1)}) %all-gather.8.cloned.1.call-update) | async-done | bytes 3670032 | tf_op jit(solution)/shard_map/all_gather | solution.py:249
  269.6 7.2 %convolution_convert_fusion.2 = bf16[1024,1024]{1,0:T(8,128)(2,1)S(1)} fusion(bf16[1024,1792]{1,0:T(8,128)(2,1)} %all-gather.8.cloned.1.call-done, bf16[1792,1024]{1,0:T(8,128)(2,1)} %param.25), kind=kOutput, calls=%fused_computation.12 | convolution fusion | flops 3759144960 | bytes 9437184 | tf_op jit(solution)/shard_map/dot_general | solution.py:251
  276.7 35.6 %all_to_all.16 = bf16[16,64,1024]{2,1,0:T(8,128)(2,1)S(1)} all-to-all(bf16[16,64,1024]{2,1,0:T(8,128)(2,1)S(1)} %bitcast.39), channel_id=1, replica_groups=mesh['req'=8,'hid'=16] {'hid'}, dimensions={0} | all-to-all | bytes 4194304 | tf_op jit(solution)/shard_map/all_to_all | solution.py:74
  312.3 0.4 convert_reduce_fusion
  312.7 0.7 add_convert_fusion.1
  (44 shorter events, 1.4 us)
Async XLA Ops:
  6.5 89.7 %copy-start = (bf16[512,1024]{1,0:T(8,128)(2,1)S(1)}, bf16[512,1024]{1,0:T(8,128)(2,1)}, u32[]{:S(2)}) copy-start(bf16[512,1024]{1,0:T(8,128)(2,1)} %param.21) | copy-start | bytes 3145732
  6.5 41.6 %all-gather.4.cloned.1.call-start = ((), (), s32[]{:S(2)}) async-start(), calls=%async_computation.4 | async-start | bytes 4718592 | tf_op jit(solution)/shard_map/all_gather | solution.py:204
  7.4 6.2 %copy-start.2 = (bf16[2,128,512]{2,1,0:T(8,128)(2,1)S(1)}, bf16[2,128,512]{2,1,0:T(8,128)(2,1)}, u32[]{:S(2)}) copy-start(bf16[2,128,512]{2,1,0:T(8,128)(2,1)} %param.13) | copy-start | bytes 786436
  12.4 2.9 copy-start.3
  12.4 2.9 copy-start.4
  13.5 82.7 %all-gather.6.cloned.1.call-start = ((), (), s32[]{:S(2)}) async-start(), calls=%async_computation.5 | async-start | bytes 2359296 | tf_op jit(solution)/shard_map/all_gather | solution.py:219
  102.5 40.4 %all-to-all-start = ((bf16[16,64,1024]{2,1,0:T(8,128)(2,1)}), bf16[16,64,1024]{2,1,0:T(8,128)(2,1)S(1)}, u32[]{:S(2)}, u32[]{:S(2)}) async-start(bf16[16,64,1024]{2,1,0:T(8,128)(2,1)} %bitcast.38), calls=%async_computation | async-start | bytes 4194304 | tf_op jit(solution)/shard_map/all_to_all | solution.py:74
  109.5 128.0 %reduce-scatter.2.cloned.1.call-start = ((), (), s32[]{:S(2)}) async-start(), calls=%async_computation.6 | async-start | bytes 8257536 | tf_op jit(solution)/shard_map/reduce_scatter | solution.py:236
  143.3 32.6 %copy-start.5 = (bf16[1024,1792]{1,0:T(8,128)(2,1)S(1)}, bf16[1024,1792]{1,0:T(8,128)(2,1)}, u32[]{:S(2)}) copy-start(bf16[1024,1792]{1,0:T(8,128)(2,1)} %param.24) | copy-start | bytes 11010052
  143.3 32.6 %copy-start.7 = (f32[1024]{0:T(1024)S(1)}, f32[1024]{0:T(1024)}, u32[]{:S(2)}) copy-start(f32[1024]{0:T(1024)} %param.22) | copy-start | bytes 12292
  175.9 5.4 %copy-start.6 = (bf16[1024,1792]{1,0:T(8,128)(2,1)S(1)}, bf16[1024,1792]{1,0:T(8,128)(2,1)}, u32[]{:S(2)}) copy-start(bf16[1024,1792]{1,0:T(8,128)(2,1)} %param.23) | copy-start | bytes 11010052
  193.4 76.1 %all-gather.8.cloned.1.call-start = ((), (), s32[]{:S(2)}) async-start(), calls=%async_computation.7 | async-start | bytes 4128768 | tf_op jit(solution)/shard_map/all_gather | solution.py:249
  269.6 43.8 %copy-start.1 = (bf16[512,1024]{1,0:T(8,128)(2,1)S(1)}, bf16[512,1024]{1,0:T(8,128)(2,1)}, u32[]{:S(2)}) copy-start(bf16[512,1024]{1,0:T(8,128)(2,1)} %param.21) | copy-start | bytes 3145732
Sparse Core Ops, SparseCore 0:
  13.6 34.5 all-gather.3
  70.9 25.2 all-gather.5
  193.6 43.9 reduce-scatter.1
  240.1 29.3 all-gather.7

commit v9 on v8

--- a/solution.py
+++ b/solution.py
@@ -105,7 +105,7 @@
     m_ref[...] = m_new
 
 
-def prefix_attention(query_flat, keys_values, q_tile=512, k_tile=4096):
+def prefix_attention(query_flat, keys_values, q_tile=1024, k_tile=4096):
     rows = query_flat.shape[0]
     length = keys_values.shape[0]
     return pl.pallas_call(

time: 320 us -> 320 us (level)
  no operation moved by 1% of the time
where the time goes in v9:
time: 320 us
  waiting for transfers between devices  146 us (46%)
  blocking collectives  79.6 us (25%)
  matrix products  25.9 us (8%)
  other arithmetic  22.9 us (7%)
  Pallas kernels  18.2 us (6%)
  between operations  13.4 us (4%)
  starting transfers between devices  7.29 us (2%)
  local copies, waits for them, and re-layouts  5.79 us (2%)
    all_to_all x1, blocking collectives, exchange_sum(): lax.all_to_all(values.reshape(count, values.shape[0] // count, values.sha...  35.6 us
    all_to_all x1, waiting for transfers between devices, exchange_sum(): lax.all_to_all(values.reshape(count, values.shape[0] // count, values.sha...  33.4 us
    all_to_all x1, blocking collectives, exchange_gather(): lax.all_to_all(jnp.broadcast_to(values[None], (count,) + values.shape), a...  31.2 us
    reduce_scatter x1, waiting for transfers between devices, on_device(): lax.psum_scatter(jnp.concatenate([gate_part.astype(jnp.bfloat16), up_part...  30.6 us
    all_gather x1, waiting for transfers between devices, on_device(): hidden_all = lax.all_gather(hidden, 'req', axis=0, tiled=True)  29.5 us
    all_gather x1, waiting for transfers between devices, on_device(): lax.all_gather(jnp.concatenate([pre_keys, pre_values], axis=1), 'req', ax...  28 us
    all_gather x1, waiting for transfers between devices, on_device(): attn_all = lax.all_gather(attn_local, 'req', axis=0, tiled=True)  24.9 us
    pallas_call x1, Pallas kernels, prefix_attention(): pl.pallas_call(prefix_kernel, out_shape=(jax.ShapeDtypeStruct((rows, 1),...  18.2 us
  transfers between devices with their start and end apart: 5, of which 5 were waited for; matrix products, arithmetic and copies ran while one was open for 2% of the time, Pallas kernels for 0%

profile of v9, /device:TPU:0, one launch (start us, length us, event | category | flops | bytes accessed | tf_op | source)
XLA Modules:
  0.0 319.6 jit_solution(6288604329697232138)
XLA Ops:
  6.6 0.8 select_reduce_fusion
  7.5 2.4 constant_dynamic-slice_fusion.1
  10.0 2.4 fusion.15
  12.4 1.0 pad_maximum_fusion.1
  13.5 0.2 all-gather.6.cloned.1.call-start
  13.7 0.2 copy.66
  13.9 0.2 copy.85
  14.1 0.2 copy.84
  14.3 0.3 multiply_cosine_fusion.1
  14.7 0.1 subtract_convert_fusion
  14.8 0.2 copy.69
  15.0 0.2 copy.70
  15.3 0.2 select_reduce_fusion.4
  15.5 0.9 dynamic-slice_convert_fusion
  16.7 0.4 fusion.45
  17.1 0.1 copy.74
  17.2 1.1 fusion.22
  18.3 0.3 copy.77
  18.8 0.1 copy.79
  18.9 0.2 reshape.334
  19.1 0.2 reshape.335
  19.3 0.9 pad_maximum_fusion.2.q_ref
  20.1 28.0 %all-gather.4.cloned.1.call-done.k_ref.v_ref = bf16[8192,256]{1,0:T(8,128)(2,1)} async-done(((bf16[1024,256]{1,0:T(8,128)(2,1)}), bf16[8192,256]{1,0:T(8,128)(2,1)}) %all-gather.4.cloned.1.call-update) | async-done | bytes 4194320 | tf_op jit(solution)/shard_map/all_gather | solution.py:204
  48.1 18.2 %shard_map.127 = (f32[1024,1]{1,0:T(8,128)}, f32[1024,1]{1,0:T(8,128)}, f32[1024,128]{1,0:T(8,128)}) custom-call(bf16[1024,128]{1,0:T(8,128)(2,1)} %pad_maximum_fusion.2.q_ref, bf16[8192,256]{1,0:T(8,128)(2,1)} %all-gather.4.cloned.1.call-done.k_ref.v_ref, bf16[8192,256]{1,0:T(8,128)(2,1)} %all-gather.4.cloned.1.call-done.k_ref.v_ref), custom_call_target="tpu_custom_call" | custom-call | tf_op jit(solution)/shard_map/pallas_call | solution.py:111
  66.3 1.7 fusion.30
  68.0 1.5 divide_convert_fusion
  69.5 0.9 reshape.325
  70.9 24.9 %all-gather.6.cloned.1.call-done = bf16[2048,512]{1,0:T(8,128)(2,1)} async-done(((bf16[256,512]{1,0:T(8,128)(2,1)}), bf16[2048,512]{1,0:T(8,128)(2,1)}) %all-gather.6.cloned.1.call-update) | async-done | bytes 2097168 | tf_op jit(solution)/shard_map/all_gather | solution.py:219
  95.8 6.3 %convolution_convert_fusion.3 = bf16[1024,1024]{1,0:T(8,128)(2,1)} fusion(bf16[512,1024]{1,0:T(8,128)(2,1)S(1)} %copy-done, bf16[2048,512]{1,0:T(8,128)(2,1)} %all-gather.6.cloned.1.call-done, s32[1024]{0:T(1024)S(1)} %add_subtract_fusion), kind=kOutput, calls=%fused_computation.13 | convolution fusion | flops 3224895488 | bytes 5246976 | tf_op jit(solution)/shard_map/dot_general | solution.py:224
  102.2 7.0 %all-to-all-start = ((bf16[16,64,1024]{2,1,0:T(8,128)(2,1)}), bf16[16,64,1024]{2,1,0:T(8,128)(2,1)S(1)}, u32[]{:S(2)}, u32[]{:S(2)}) async-start(bf16[16,64,1024]{2,1,0:T(8,128)(2,1)} %bitcast.38), calls=%async_computation | async-start | bytes 4194304 | tf_op jit(solution)/shard_map/all_to_all | solution.py:74
  109.2 33.4 %all-to-all-done = bf16[16,64,1024]{2,1,0:T(8,128)(2,1)S(1)} async-done(((bf16[16,64,1024]{2,1,0:T(8,128)(2,1)}), bf16[16,64,1024]{2,1,0:T(8,128)(2,1)S(1)}, u32[]{:S(2)}, u32[]{:S(2)}) %all-to-all-start) | async-done | bytes 2097184 | tf_op jit(solution)/shard_map/all_to_all | solution.py:74
  142.6 0.4 convert_reduce_fusion.1
  143.0 1.1 add_convert_fusion.2
  144.1 0.3 broadcast_in_dim.12
  144.3 31.2 %all_to_all.15 = bf16[16,64,1024]{2,1,0:T(8,128)(2,1)S(1)} all-to-all(bf16[16,64,1024]{2,1,0:T(8,128)(2,1)S(1)} %broadcast_in_dim.12), channel_id=1, replica_groups=mesh['req'=8,'hid'=16] {'hid'}, dimensions={0} | all-to-all | bytes 4194304 | tf_op jit(solution)/shard_map/all_to_all | solution.py:81
  175.5 5.4 %convolution_convert_fusion = bf16[1024,1792]{1,0:T(8,128)(2,1)} fusion(bf16[1024,1792]{1,0:T(8,128)(2,1)S(1)} %copy-done.5, bf16[1024,1024]{1,0:T(8,128)(2,1)S(1)} %bitcast.34, f32[1024]{0:T(1024)S(1)} %copy-done.7), kind=kOutput, calls=%fused_computation.10 | convolution fusion | flops 3763077120 | bytes 9441280 | tf_op jit(solution)/shard_map/dot_general | solution.py:233
  181.0 5.4 %convolution_convert_fusion.1 = bf16[1024,1792]{1,0:T(8,128)(2,1)} fusion(bf16[1024,1792]{1,0:T(8,128)(2,1)S(1)} %copy-done.6, bf16[1024,1024]{1,0:T(8,128)(2,1)S(1)} %bitcast.35, f32[1024]{0:T(1024)S(1)} %copy-done.7), kind=kOutput, calls=%fused_computation.11 | convolution fusion | flops 3763077120 | bytes 9441280 | tf_op jit(solution)/shard_map/dot_general | solution.py:232
  186.4 6.6 %pad_maximum_fusion = bf16[1024,3584]{1,0:T(8,128)(2,1)} fusion(bf16[1024,1792]{1,0:T(8,128)(2,1)} %convolution_convert_fusion, bf16[1024,1792]{1,0:T(8,128)(2,1)} %convolution_convert_fusion.1), kind=kLoop, calls=%fused_computation.2 | loop fusion | flops 14680064 | bytes 14680064 | tf_op jit(solution)/shard_map/concatenate | solution.py:237
  193.1 0.5 fusion.2
  193.6 12.9 %psum.7 = f32[1024]{0:T(1024)S(1)} all-reduce(f32[1024]{0:T(1024)S(1)} %fusion.2), channel_id=1, replica_groups=mesh['req'=8,'hid'=16] {'req'}, use_global_device_ids=true, to_apply=%region_12.13 | all-reduce | flops 1024 | bytes 8192 | tf_op jit(solution)/shard_map/psum | solution.py:234
  206.6 30.6 %reduce-scatter.2.cloned.1.call-done = bf16[128,3584]{1,0:T(8,128)(2,1)} async-done(((bf16[1024,3584]{1,0:T(8,128)(2,1)}), bf16[128,3584]{1,0:T(8,128)(2,1)}) %reduce-scatter.2.cloned.1.call-update) | async-done | bytes 917520 | tf_op jit(solution)/shard_map/reduce_scatter | solution.py:236
  237.1 1.4 convert_element_type.123
  238.5 1.1 fusion.9
  239.6 29.5 %all-gather.8.cloned.1.call-done = bf16[1024,1792]{1,0:T(8,128)(2,1)} async-done(((bf16[128,1792]{1,0:T(8,128)(2,1)}), bf16[1024,1792]{1,0:T(8,128)(2,1)}) %all-gather.8.cloned.1.call-update) | async-done | bytes 3670032 | tf_op jit(solution)/shard_map/all_gather | solution.py:249
  269.2 7.2 %convolution_convert_fusion.2 = bf16[1024,1024]{1,0:T(8,128)(2,1)S(1)} fusion(bf16[1024,1792]{1,0:T(8,128)(2,1)} %all-gather.8.cloned.1.call-done, bf16[1792,1024]{1,0:T(8,128)(2,1)} %param.25), kind=kOutput, calls=%fused_computation.12 | convolution fusion | flops 3759144960 | bytes 9437184 | tf_op jit(solution)/shard_map/dot_general | solution.py:251
  276.4 35.6 %all_to_all.16 = bf16[16,64,1024]{2,1,0:T(8,128)(2,1)S(1)} all-to-all(bf16[16,64,1024]{2,1,0:T(8,128)(2,1)S(1)} %bitcast.39), channel_id=1, replica_groups=mesh['req'=8,'hid'=16] {'hid'}, dimensions={0} | all-to-all | bytes 4194304 | tf_op jit(solution)/shard_map/all_to_all | solution.py:74
  311.9 0.4 convert_reduce_fusion
  312.3 0.7 add_convert_fusion.1
  (44 shorter events, 1.3 us)
Async XLA Ops:
  6.5 89.3 %copy-start = (bf16[512,1024]{1,0:T(8,128)(2,1)S(1)}, bf16[512,1024]{1,0:T(8,128)(2,1)}, u32[]{:S(2)}) copy-start(bf16[512,1024]{1,0:T(8,128)(2,1)} %param.21) | copy-start | bytes 3145732
  6.5 41.6 %all-gather.4.cloned.1.call-start = ((), (), s32[]{:S(2)}) async-start(), calls=%async_computation.4 | async-start | bytes 4718592 | tf_op jit(solution)/shard_map/all_gather | solution.py:204
  7.4 6.2 %copy-start.2 = (bf16[2,128,512]{2,1,0:T(8,128)(2,1)S(1)}, bf16[2,128,512]{2,1,0:T(8,128)(2,1)}, u32[]{:S(2)}) copy-start(bf16[2,128,512]{2,1,0:T(8,128)(2,1)} %param.13) | copy-start | bytes 786436
  12.4 2.9 copy-start.3
  12.4 2.9 copy-start.4
  13.5 82.4 %all-gather.6.cloned.1.call-start = ((), (), s32[]{:S(2)}) async-start(), calls=%async_computation.5 | async-start | bytes 2359296 | tf_op jit(solution)/shard_map/all_gather | solution.py:219
  102.2 40.4 %all-to-all-start = ((bf16[16,64,1024]{2,1,0:T(8,128)(2,1)}), bf16[16,64,1024]{2,1,0:T(8,128)(2,1)S(1)}, u32[]{:S(2)}, u32[]{:S(2)}) async-start(bf16[16,64,1024]{2,1,0:T(8,128)(2,1)} %bitcast.38), calls=%async_computation | async-start | bytes 4194304 | tf_op jit(solution)/shard_map/all_to_all | solution.py:74
  109.2 128.0 %reduce-scatter.2.cloned.1.call-start = ((), (), s32[]{:S(2)}) async-start(), calls=%async_computation.6 | async-start | bytes 8257536 | tf_op jit(solution)/shard_map/reduce_scatter | solution.py:236
  143.0 32.6 %copy-start.5 = (bf16[1024,1792]{1,0:T(8,128)(2,1)S(1)}, bf16[1024,1792]{1,0:T(8,128)(2,1)}, u32[]{:S(2)}) copy-start(bf16[1024,1792]{1,0:T(8,128)(2,1)} %param.24) | copy-start | bytes 11010052
  143.0 32.5 %copy-start.7 = (f32[1024]{0:T(1024)S(1)}, f32[1024]{0:T(1024)}, u32[]{:S(2)}) copy-start(f32[1024]{0:T(1024)} %param.22) | copy-start | bytes 12292
  175.5 5.4 %copy-start.6 = (bf16[1024,1792]{1,0:T(8,128)(2,1)S(1)}, bf16[1024,1792]{1,0:T(8,128)(2,1)}, u32[]{:S(2)}) copy-start(bf16[1024,1792]{1,0:T(8,128)(2,1)} %param.23) | copy-start | bytes 11010052
  193.1 76.1 %all-gather.8.cloned.1.call-start = ((), (), s32[]{:S(2)}) async-start(), calls=%async_computation.7 | async-start | bytes 4128768 | tf_op jit(solution)/shard_map/all_gather | solution.py:249
  269.2 43.8 %copy-start.1 = (bf16[512,1024]{1,0:T(8,128)(2,1)S(1)}, bf16[512,1024]{1,0:T(8,128)(2,1)}, u32[]{:S(2)}) copy-start(bf16[512,1024]{1,0:T(8,128)(2,1)} %param.21) | copy-start | bytes 3145732
Sparse Core Ops, SparseCore 0:
  13.6 34.5 all-gather.3
  70.6 25.2 all-gather.5
  193.2 43.9 reduce-scatter.1
  239.8 29.3 all-gather.7
